TPU v7x, 256 devices: a whole 4x4x8 slice. The times are simulated.
256 devices in a mesh: seg: 8 (over z), blk: 32 (over x, y, core).
Axes of the slice: x: 4, y: 4, z: 8, core: 2. Of those that a mesh axis runs over, the one named last changes fastest.
Arguments:
- sampled_data: float32 [4, 256, 65536], P(None, None, ('seg', 'blk')), may hold values from -6 to 6
- update_weights: float32 [4, 256, 256], replicated, may hold values from -0.375 to 0.375
- eigenbasis_columns: float32 [4, 256, 256], replicated, may hold values from -0.375 to 0.375
- measuring_operator: float32 [4, 256, 256], replicated, may hold values from -0.375 to 0.375
- eigen_damping: float32 [256, 4, 128], P(('seg', 'blk')), may hold values from 0 to 1, as said below
- backward_damping: float32 [256, 4, 128], P(('seg', 'blk')), may hold values from 0 to 1, as said below
- rotation_angle: float32 [256, 4, 128], P(('seg', 'blk')), may hold values from 0.0105 to 0.21
- switch_flags: int32 [65536], P(('seg', 'blk')), may hold values 0 or 1
- prior_expectation: float32 [2, 4, 128], replicated, may hold values from -6 to 6
Outputs:
- states: bfloat16 [4, 256, 65536], P(None, None, ('seg', 'blk'))
- fitted: bfloat16 [4, 256, 65536], P(None, None, ('seg', 'blk'))
Inputs may be any that keep to these rules, and one draw needn't show every extreme that they name: `eigen_damping`: positive decay rates per step. `backward_damping`: positive decay rates per step.
All inputs are finite; a program needn't handle non-finite values. No bound on the sum of `switch_flags` on one device may be relied on, other than what follows from the above.
Results may differ from a plain program's by a relative error of at most 0.0055.
Values sent between devices are 32-bit elements; how exact they have to be, the bound alone decides.
No kernel may reach another device: no remote copies, remote signals or barrier semaphores. Data moves between devices by JAX's collectives and lax.ppermute only.
A program may use at most 64 MiB of HBM per device.

v0:
```python
import math

import jax
import jax.numpy as jnp
from jax import lax
from jax.sharding import PartitionSpec as P

spike_multiplier = 0.7


def entering_2(part, axis, combine, identity, reverse):
    count = lax.axis_size(axis)
    place = lax.axis_index(axis)
    ahead = count - 1 - place if reverse else place
    gathered = lax.all_gather(part, axis)
    state = jnp.zeros_like(part) + jnp.asarray(identity, part.dtype)

    def one(turn, state):
        source = count - 1 - turn if reverse else turn
        return combine(state, lax.dynamic_index_in_dim(gathered, source, 0, False))

    return lax.fori_loop(0, ahead, one, state)


def broadcast(block, axis, owner):
    block = jnp.where(lax.axis_index(axis) == owner, block, jnp.zeros_like(block))
    return lax.psum(block, axis)


def shifted(block, axis, distance):
    devices = range(lax.axis_size(axis))
    route = [(i - distance, i) for i in devices if i - distance in devices]
    return lax.ppermute(block, axis, route)


def compose(earlier, latter):
    growth_real, growth_imag, offset_real, offset_imag = earlier
    factor_real, factor_imag, addend_real, addend_imag = latter
    return (
        factor_real * growth_real - factor_imag * growth_imag,
        factor_real * growth_imag + factor_imag * growth_real,
        factor_real * offset_real - factor_imag * offset_imag + addend_real,
        factor_real * offset_imag + factor_imag * offset_real + addend_imag,
    )


def split_parts(element):
    return tuple((element[..., member, :, :] for member in range(4)))


def join_parts(earlier, latter):
    return jnp.stack(compose(split_parts(earlier), split_parts(latter)), axis=-3)


def prefix(element, reverse):
    neutral = jnp.concatenate([jnp.ones_like(element[:1]), jnp.zeros_like(element[1:])], axis=0)
    block_count = lax.axis_size("blk")
    inside = entering_2(element, "blk", join_parts, neutral, reverse)
    through = join_parts(inside, element)
    whole_block = broadcast(through, "blk", 0 if reverse else block_count - 1)
    segment_count = lax.axis_size("seg")
    shift_by = -1 if reverse else 1
    edge_device = lax.axis_index("seg") == (segment_count - 1 if reverse else 0)

    def advance(turn_index, outside):
        reached = join_parts(outside, whole_block)
        passed = shifted(reached, "seg", shift_by)
        return jnp.where(edge_device, neutral, passed)

    outside = lax.fori_loop(0, segment_count - 1, advance, neutral)
    return join_parts(outside, inside)


def on_device(
    sampled_data,
    update_weights,
    eigenbasis_columns,
    measuring_operator,
    eigen_damping,
    backward_damping,
    rotation_angle,
    switch_flags,
    prior_expectation,
):
    highest = lax.Precision.HIGHEST
    mode_count = eigen_damping.shape[2]
    step_count = sampled_data.shape[2]
    jolt_moment = switch_flags == 1
    multiplier = jnp.where(jolt_moment, spike_multiplier, 1.0).astype(jnp.float32)[:, None, None]
    logarithm_multiplier = jnp.where(jolt_moment, math.log(spike_multiplier), 0.0).astype(
        jnp.float32
    )[:, None, None]
    forward_rate = eigen_damping[0]
    backward_rate = backward_damping[0]
    angle = rotation_angle[0]
    drive = jnp.einsum("asm,amt->tas", update_weights, sampled_data, precision=highest)
    scaling = jnp.sqrt(-jnp.expm1(-2.0 * forward_rate))[None]
    magnitude = jnp.exp(-forward_rate)
    growth_real = (magnitude * jnp.cos(angle))[None] * multiplier
    growth_imag = (magnitude * jnp.sin(angle))[None] * multiplier
    local_scan = lax.associative_scan(
        compose,
        (
            growth_real,
            growth_imag,
            scaling * drive[:, :, :mode_count],
            scaling * drive[:, :, mode_count:],
        ),
        axis=0,
    )
    element = jnp.stack([member[-1] for member in local_scan], axis=0)
    carried = prefix(element, False)
    carry_real = (
        carried[0] * prior_expectation[0] - carried[1] * prior_expectation[1] + carried[2]
    )[None]
    carry_imag = (
        carried[0] * prior_expectation[1] + carried[1] * prior_expectation[0] + carried[3]
    )[None]
    mean_real = local_scan[0] * carry_real - local_scan[1] * carry_imag + local_scan[2]
    mean_imag = local_scan[0] * carry_imag + local_scan[1] * carry_real + local_scan[3]
    last_device = (lax.axis_index("seg") == lax.axis_size("seg") - 1) & (
        lax.axis_index("blk") == lax.axis_size("blk") - 1
    )
    columns = lax.broadcasted_iota(jnp.int32, (step_count,), 0)
    final_step = (last_device & (columns == step_count - 1))[:, None, None]
    smooth_magnitude = jnp.exp(-backward_rate)
    back_real = jnp.where(final_step, 0.0, (smooth_magnitude * jnp.cos(angle))[None] * multiplier)
    back_imag = jnp.where(final_step, 0.0, -(smooth_magnitude * jnp.sin(angle))[None] * multiplier)
    weight = jnp.where(
        final_step,
        1.0,
        -jnp.expm1(2.0 * logarithm_multiplier - (forward_rate + backward_rate)[None]),
    )
    back_scan = lax.associative_scan(
        compose,
        (back_real, back_imag, weight * mean_real, weight * mean_imag),
        reverse=True,
        axis=0,
    )
    back_element = jnp.stack([member[0] for member in back_scan], axis=0)
    entering = prefix(back_element, True)
    entry_real = entering[2][None]
    entry_imag = entering[3][None]
    smooth_real = back_scan[0] * entry_real - back_scan[1] * entry_imag + back_scan[2]
    smooth_imag = back_scan[0] * entry_imag + back_scan[1] * entry_real + back_scan[3]
    stacked = jnp.concatenate([smooth_real, smooth_imag], axis=2)
    states = jnp.einsum("ars,tas->art", eigenbasis_columns, stacked, precision=highest).astype(
        jnp.bfloat16
    )
    fitted = (
        sampled_data - jnp.einsum("ams,tas->amt", measuring_operator, stacked, precision=highest)
    ).astype(jnp.bfloat16)
    return (states, fitted)


def solution(mesh):
    placed = (
        P(None, None, ("seg", "blk")),
        P(),
        P(),
        P(),
        P(("seg", "blk"), None, None),
        P(("seg", "blk"), None, None),
        P(("seg", "blk"), None, None),
        P(("seg", "blk")),
        P(),
    )
    return jax.shard_map(
        on_device,
        mesh=mesh,
        in_specs=placed,
        out_specs=(P(None, None, ("seg", "blk")), P(None, None, ("seg", "blk"))),
        check_vma=False,
    )
```

profile of v0, /device:TPU:96, one launch (start us, length us, event | category | flops | bytes accessed | tf_op | source)
XLA Modules:
  0.0 456.6 jit_solution(1998842729210139785)
XLA Ops:
  6.0 3.2 convolution_bitcast_fusion.1
  16.1 1.8 slice.1343
  17.9 1.7 slice.1340
  20.3 1.7 slice.1346
  22.1 1.7 slice.1342
  26.8 1.6 multiply_subtract_fusion.5
  51.3 1.9 pad.447
  54.2 1.5 pad.479
  61.9 2.0 pad.450
  63.9 2.0 pad.448
  65.9 2.0 pad.449
  67.9 2.0 pad.451
  79.4 1.9 pad.454
  81.4 3.9 pad.452
  85.2 3.8 pad.453
  89.8 2.2 pad.455
  92.7 1.8 pad.484
  94.5 3.8 pad.485
  99.1 2.2 pad.487
  102.0 25.2 %all-gather = f32[128,4,128]{2,1,0:T(4,128)S(1)} all-gather(f32[4,4,128]{2,1,0:T(4,128)S(1)} %copy.36), channel_id=2, replica_groups=mesh['seg'=8,'blk'=32] {'blk'}, dimensions={0}, use_global_device_ids=true | all-gather | bytes 270336 | tf_op jit(solution)/shard_map/all_gather | solution.py:15
  127.3 68.3 %psum.14 = f32[4,4,128]{2,0,1:T(4,128)S(1)} all-reduce(f32[4,4,128]{2,0,1:T(4,128)S(1)} %maximum_select_fusion), channel_id=1, replica_groups=mesh['seg'=8,'blk'=32] {'blk'}, use_global_device_ids=true, to_apply=%region_2.3 | all-reduce | flops 2048 | bytes 16384 | tf_op jit(solution)/shard_map/psum | solution.py:27
  196.2 47.1 %while.43 = (s32[]{:T(128)}, f32[4,4,128]{2,1,0:T(4,128)S(1)}, pred[]{:T(512)}, f32[4,4,128]{2,1,0:T(4,128)S(1)}, s32[]{:T(128)}, /*index=5*/f32[4,4,128]{2,1,0:T(4,128)S(1)}) while((s32[]{:T(128)}, f32[4,4,128]{2,1,0:T(4,128)S(1)}, pred[]{:T(512)}, f32[4,4,128]{2,1,0:T(4,128)S(1)}, s32[]{:T(128)}, ...), condition=%wide.region_4.5_spmd, body=%wide.region_3.4_spmd.sunk | while | flops 15362 | bytes 98414 | solution.py:70
  196.3 5.0 %collective-permute-start = (f32[4,4,128]{2,1,0:T(4,128)S(1)}, f32[4,4,128]{2,1,0:T(4,128)S(1)}, u32[]{:S(2)}, u32[]{:S(2)}) collective-permute-start(f32[4,4,128]{2,1,0:T(4,128)S(1)} %pad_maximum_fusion.70), channel_id=1, source_target_pairs={{0,32},{32,64},{64,96},{96,128},{128,160},{160,192},{192,224},{1,3... | collective-permute-start | bytes 24584 | tf_op jit(solution)/shard_map/while/body/eval_jaxpr/ppermute | solution.py:33
  201.3 1.3 collective-permute-done
  202.7 5.4 %collective-permute-start = (f32[4,4,128]{2,1,0:T(4,128)S(1)}, f32[4,4,128]{2,1,0:T(4,128)S(1)}, u32[]{:S(2)}, u32[]{:S(2)}) collective-permute-start(f32[4,4,128]{2,1,0:T(4,128)S(1)} %pad_maximum_fusion.70), channel_id=1, source_target_pairs={{0,32},{32,64},{64,96},{96,128},{128,160},{160,192},{192,224},{1,3... | collective-permute-start | bytes 24584 | tf_op jit(solution)/shard_map/while/body/eval_jaxpr/ppermute | solution.py:33
  208.1 1.3 collective-permute-done
  209.5 5.4 %collective-permute-start = (f32[4,4,128]{2,1,0:T(4,128)S(1)}, f32[4,4,128]{2,1,0:T(4,128)S(1)}, u32[]{:S(2)}, u32[]{:S(2)}) collective-permute-start(f32[4,4,128]{2,1,0:T(4,128)S(1)} %pad_maximum_fusion.70), channel_id=1, source_target_pairs={{0,32},{32,64},{64,96},{96,128},{128,160},{160,192},{192,224},{1,3... | collective-permute-start | bytes 24584 | tf_op jit(solution)/shard_map/while/body/eval_jaxpr/ppermute | solution.py:33
  214.9 1.3 collective-permute-done
  216.2 5.4 %collective-permute-start = (f32[4,4,128]{2,1,0:T(4,128)S(1)}, f32[4,4,128]{2,1,0:T(4,128)S(1)}, u32[]{:S(2)}, u32[]{:S(2)}) collective-permute-start(f32[4,4,128]{2,1,0:T(4,128)S(1)} %pad_maximum_fusion.70), channel_id=1, source_target_pairs={{0,32},{32,64},{64,96},{96,128},{128,160},{160,192},{192,224},{1,3... | collective-permute-start | bytes 24584 | tf_op jit(solution)/shard_map/while/body/eval_jaxpr/ppermute | solution.py:33
  221.7 1.3 collective-permute-done
  223.0 5.4 %collective-permute-start = (f32[4,4,128]{2,1,0:T(4,128)S(1)}, f32[4,4,128]{2,1,0:T(4,128)S(1)}, u32[]{:S(2)}, u32[]{:S(2)}) collective-permute-start(f32[4,4,128]{2,1,0:T(4,128)S(1)} %pad_maximum_fusion.70), channel_id=1, source_target_pairs={{0,32},{32,64},{64,96},{96,128},{128,160},{160,192},{192,224},{1,3... | collective-permute-start | bytes 24584 | tf_op jit(solution)/shard_map/while/body/eval_jaxpr/ppermute | solution.py:33
  228.4 1.3 collective-permute-done
  229.8 5.4 %collective-permute-start = (f32[4,4,128]{2,1,0:T(4,128)S(1)}, f32[4,4,128]{2,1,0:T(4,128)S(1)}, u32[]{:S(2)}, u32[]{:S(2)}) collective-permute-start(f32[4,4,128]{2,1,0:T(4,128)S(1)} %pad_maximum_fusion.70), channel_id=1, source_target_pairs={{0,32},{32,64},{64,96},{96,128},{128,160},{160,192},{192,224},{1,3... | collective-permute-start | bytes 24584 | tf_op jit(solution)/shard_map/while/body/eval_jaxpr/ppermute | solution.py:33
  236.6 5.4 %collective-permute-start = (f32[4,4,128]{2,1,0:T(4,128)S(1)}, f32[4,4,128]{2,1,0:T(4,128)S(1)}, u32[]{:S(2)}, u32[]{:S(2)}) collective-permute-start(f32[4,4,128]{2,1,0:T(4,128)S(1)} %pad_maximum_fusion.70), channel_id=1, source_target_pairs={{0,32},{32,64},{64,96},{96,128},{128,160},{160,192},{192,224},{1,3... | collective-permute-start | bytes 24584 | tf_op jit(solution)/shard_map/while/body/eval_jaxpr/ppermute | solution.py:33
  244.8 2.7 add_multiply_fusion.1
  248.8 1.4 slice.1502
  251.0 1.7 slice.1428
  253.0 1.4 slice.1506
  255.9 1.8 slice.1430
  260.2 2.9 slice.1188
  267.6 1.4 multiply_subtract_fusion.7
  289.6 2.0 pad.419
  300.3 4.8 %rev.16 = f32[256,4,128]{2,0,1:T(8,128)} reverse(f32[256,4,128]{2,0,1:T(8,128)} %add.1037), dimensions={0} | reverse | bytes 1048576 | tf_op jit(solution)/shard_map/rev | solution.py:134
  305.3 2.6 rev.17
  309.0 2.6 rev.18
  311.9 2.6 rev.19
  314.5 22.1 %all-gather.1 = f32[128,4,128]{2,1,0:T(4,128)S(1)} all-gather(f32[4,4,128]{2,1,0:T(4,128)S(1)} %copy.48), channel_id=3, replica_groups=mesh['seg'=8,'blk'=32] {'blk'}, dimensions={0}, use_global_device_ids=true | all-gather | bytes 270336 | tf_op jit(solution)/shard_map/all_gather | solution.py:15
  336.6 1.7 while.44
  338.4 64.6 %psum.15 = f32[4,4,128]{2,0,1:T(4,128)S(1)} all-reduce(f32[4,4,128]{2,0,1:T(4,128)S(1)} %maximum_select_fusion.1), channel_id=1, replica_groups=mesh['seg'=8,'blk'=32] {'blk'}, use_global_device_ids=true, to_apply=%region_7.8 | all-reduce | flops 2048 | bytes 16384 | tf_op jit(solution)/shard_map/psum | solution.py:27
  403.0 47.8 %while.45 = (s32[]{:T(128)}, f32[4,4,128]{2,1,0:T(4,128)S(1)}, pred[]{:T(512)}, f32[4,4,128]{2,1,0:T(4,128)S(1)}, s32[]{:T(128)}, /*index=5*/f32[4,4,128]{2,1,0:T(4,128)S(1)}) while((s32[]{:T(128)}, f32[4,4,128]{2,1,0:T(4,128)S(1)}, pred[]{:T(512)}, f32[4,4,128]{2,1,0:T(4,128)S(1)}, s32[]{:T(128)}, ...), condition=%wide.region_9.10_spmd, body=%wide.region_8.9_spmd.sunk | while | flops 15362 | bytes 98414 | solution.py:70
  403.0 1.9 collective-permute-start.1
  405.0 5.1 %collective-permute-done.1 = f32[4,4,128]{2,1,0:T(4,128)S(1)} collective-permute-done((f32[4,4,128]{2,1,0:T(4,128)S(1)}, f32[4,4,128]{2,1,0:T(4,128)S(1)}, u32[]{:S(2)}, u32[]{:S(2)}) %collective-permute-start.1) | collective-permute-done | bytes 8224 | tf_op jit(solution)/shard_map/while/body/eval_jaxpr/ppermute | solution.py:33
  410.1 1.9 collective-permute-start.1
  412.0 4.8 %collective-permute-done.1 = f32[4,4,128]{2,1,0:T(4,128)S(1)} collective-permute-done((f32[4,4,128]{2,1,0:T(4,128)S(1)}, f32[4,4,128]{2,1,0:T(4,128)S(1)}, u32[]{:S(2)}, u32[]{:S(2)}) %collective-permute-start.1) | collective-permute-done | bytes 8224 | tf_op jit(solution)/shard_map/while/body/eval_jaxpr/ppermute | solution.py:33
  416.9 1.9 collective-permute-start.1
  418.8 4.8 %collective-permute-done.1 = f32[4,4,128]{2,1,0:T(4,128)S(1)} collective-permute-done((f32[4,4,128]{2,1,0:T(4,128)S(1)}, f32[4,4,128]{2,1,0:T(4,128)S(1)}, u32[]{:S(2)}, u32[]{:S(2)}) %collective-permute-start.1) | collective-permute-done | bytes 8224 | tf_op jit(solution)/shard_map/while/body/eval_jaxpr/ppermute | solution.py:33
  423.6 1.9 collective-permute-start.1
  425.6 4.8 %collective-permute-done.1 = f32[4,4,128]{2,1,0:T(4,128)S(1)} collective-permute-done((f32[4,4,128]{2,1,0:T(4,128)S(1)}, f32[4,4,128]{2,1,0:T(4,128)S(1)}, u32[]{:S(2)}, u32[]{:S(2)}) %collective-permute-start.1) | collective-permute-done | bytes 8224 | tf_op jit(solution)/shard_map/while/body/eval_jaxpr/ppermute | solution.py:33
  430.4 1.9 collective-permute-start.1
  432.4 4.8 %collective-permute-done.1 = f32[4,4,128]{2,1,0:T(4,128)S(1)} collective-permute-done((f32[4,4,128]{2,1,0:T(4,128)S(1)}, f32[4,4,128]{2,1,0:T(4,128)S(1)}, u32[]{:S(2)}, u32[]{:S(2)}) %collective-permute-start.1) | collective-permute-done | bytes 8224 | tf_op jit(solution)/shard_map/while/body/eval_jaxpr/ppermute | solution.py:33
  437.2 1.9 collective-permute-start.1
  439.1 4.8 %collective-permute-done.1 = f32[4,4,128]{2,1,0:T(4,128)S(1)} collective-permute-done((f32[4,4,128]{2,1,0:T(4,128)S(1)}, f32[4,4,128]{2,1,0:T(4,128)S(1)}, u32[]{:S(2)}, u32[]{:S(2)}) %collective-permute-start.1) | collective-permute-done | bytes 8224 | tf_op jit(solution)/shard_map/while/body/eval_jaxpr/ppermute | solution.py:33
  444.0 1.9 collective-permute-start.1
  445.9 4.8 %collective-permute-done.1 = f32[4,4,128]{2,1,0:T(4,128)S(1)} collective-permute-done((f32[4,4,128]{2,1,0:T(4,128)S(1)}, f32[4,4,128]{2,1,0:T(4,128)S(1)}, u32[]{:S(2)}, u32[]{:S(2)}) %collective-permute-start.1) | collective-permute-done | bytes 8224 | tf_op jit(solution)/shard_map/while/body/eval_jaxpr/ppermute | solution.py:33
  (787 shorter events, 109.5 us)
Async XLA Ops:
  0.6 5.3 %copy-start = (f32[4,256,256]{2,1,0:T(8,128)S(1)}, f32[4,256,256]{2,1,0:T(8,128)}, u32[]{:S(2)}) copy-start(f32[4,256,256]{2,1,0:T(8,128)} %param.18) | copy-start | bytes 3145732
  0.7 0.8 copy-start.83
  1.4 8.1 %copy-start.78 = (pred[256]{0:T(512)(128)(4,1)}, pred[256]{0:T(512)(128)(4,1)S(1)}, u32[]{:S(2)}) copy-start(pred[256]{0:T(512)(128)(4,1)S(1)} %compare_and_fusion) | copy-start | bytes 772
  6.0 3.2 copy-start.2
  9.8 1.9 copy-start.3
  9.8 2.4 copy-start.5
  9.8 3.0 copy-start.7
  9.8 3.0 copy-start.9
  12.3 2.3 copy-start.4
  13.4 1.9 copy-start.10
  16.1 3.4 copy-start.8
  20.3 3.4 copy-start.6
  36.3 1.0 copy-start.38
  36.3 1.0 copy-start.39
  45.5 0.8 copy-start.47
  45.6 0.8 copy-start.46
  51.3 1.9 copy-start.48
  53.3 0.8 copy-start.45
  54.1 1.5 copy-start.26
  58.7 1.0 copy-start.27
  67.9 2.0 copy-start.42
  69.9 0.9 copy-start.37
  70.8 0.9 copy-start.36
  73.7 2.1 copy-start.13
  73.7 2.1 copy-start.14
  73.7 2.1 copy-start.15
  75.1 1.0 copy-start.11
  75.1 1.1 copy-start.12
  77.8 0.8 copy-start.55
  79.4 21.9 %copy-start.17 = (f32[256,4,128]{2,0,1:T(8,128)}, f32[256,4,128]{2,0,1:T(8,128)S(1)}, u32[]{:S(2)}) copy-start(f32[256,4,128]{2,0,1:T(8,128)S(1)} %pad.486) | copy-start | bytes 1572868
  81.4 10.6 %copy-start.18 = (f32[256,4,128]{2,0,1:T(8,128)}, f32[256,4,128]{2,0,1:T(8,128)S(1)}, u32[]{:S(2)}) copy-start(f32[256,4,128]{2,0,1:T(8,128)S(1)} %pad.454) | copy-start | bytes 1572868
  94.5 6.8 %copy-start.19 = (f32[256,4,128]{2,0,1:T(8,128)}, f32[256,4,128]{2,0,1:T(8,128)S(1)}, u32[]{:S(2)}) copy-start(f32[256,4,128]{2,0,1:T(8,128)S(1)} %pad.484) | copy-start | bytes 1572868
  94.5 4.5 copy-start.32
  102.0 25.2 %copy-start.25 = (f32[4,4,128]{2,1,0:T(4,128)S(1)}, f32[4,4,128]{2,1,0:T(4,128)}, u32[]{:S(2)}) copy-start(f32[4,4,128]{2,1,0:T(4,128)} %constant.74.clone.1) | copy-start | bytes 24580
  196.3 6.4 %collective-permute-start = (f32[4,4,128]{2,1,0:T(4,128)S(1)}, f32[4,4,128]{2,1,0:T(4,128)S(1)}, u32[]{:S(2)}, u32[]{:S(2)}) collective-permute-start(f32[4,4,128]{2,1,0:T(4,128)S(1)} %pad_maximum_fusion.70), channel_id=1, source_target_pairs={{0,32},{32,64},{64,96},{96,128},{128,160},{160,192},{192,224},{1,3... | collective-permute-start | bytes 24584 | tf_op jit(solution)/shard_map/while/body/eval_jaxpr/ppermute | solution.py:33
  202.7 6.8 %collective-permute-start = (f32[4,4,128]{2,1,0:T(4,128)S(1)}, f32[4,4,128]{2,1,0:T(4,128)S(1)}, u32[]{:S(2)}, u32[]{:S(2)}) collective-permute-start(f32[4,4,128]{2,1,0:T(4,128)S(1)} %pad_maximum_fusion.70), channel_id=1, source_target_pairs={{0,32},{32,64},{64,96},{96,128},{128,160},{160,192},{192,224},{1,3... | collective-permute-start | bytes 24584 | tf_op jit(solution)/shard_map/while/body/eval_jaxpr/ppermute | solution.py:33
  209.5 6.8 %collective-permute-start = (f32[4,4,128]{2,1,0:T(4,128)S(1)}, f32[4,4,128]{2,1,0:T(4,128)S(1)}, u32[]{:S(2)}, u32[]{:S(2)}) collective-permute-start(f32[4,4,128]{2,1,0:T(4,128)S(1)} %pad_maximum_fusion.70), channel_id=1, source_target_pairs={{0,32},{32,64},{64,96},{96,128},{128,160},{160,192},{192,224},{1,3... | collective-permute-start | bytes 24584 | tf_op jit(solution)/shard_map/while/body/eval_jaxpr/ppermute | solution.py:33
  216.2 6.8 %collective-permute-start = (f32[4,4,128]{2,1,0:T(4,128)S(1)}, f32[4,4,128]{2,1,0:T(4,128)S(1)}, u32[]{:S(2)}, u32[]{:S(2)}) collective-permute-start(f32[4,4,128]{2,1,0:T(4,128)S(1)} %pad_maximum_fusion.70), channel_id=1, source_target_pairs={{0,32},{32,64},{64,96},{96,128},{128,160},{160,192},{192,224},{1,3... | collective-permute-start | bytes 24584 | tf_op jit(solution)/shard_map/while/body/eval_jaxpr/ppermute | solution.py:33
  223.0 6.8 %collective-permute-start = (f32[4,4,128]{2,1,0:T(4,128)S(1)}, f32[4,4,128]{2,1,0:T(4,128)S(1)}, u32[]{:S(2)}, u32[]{:S(2)}) collective-permute-start(f32[4,4,128]{2,1,0:T(4,128)S(1)} %pad_maximum_fusion.70), channel_id=1, source_target_pairs={{0,32},{32,64},{64,96},{96,128},{128,160},{160,192},{192,224},{1,3... | collective-permute-start | bytes 24584 | tf_op jit(solution)/shard_map/while/body/eval_jaxpr/ppermute | solution.py:33
  229.8 6.8 %collective-permute-start = (f32[4,4,128]{2,1,0:T(4,128)S(1)}, f32[4,4,128]{2,1,0:T(4,128)S(1)}, u32[]{:S(2)}, u32[]{:S(2)}) collective-permute-start(f32[4,4,128]{2,1,0:T(4,128)S(1)} %pad_maximum_fusion.70), channel_id=1, source_target_pairs={{0,32},{32,64},{64,96},{96,128},{128,160},{160,192},{192,224},{1,3... | collective-permute-start | bytes 24584 | tf_op jit(solution)/shard_map/while/body/eval_jaxpr/ppermute | solution.py:33
  236.6 6.8 %collective-permute-start = (f32[4,4,128]{2,1,0:T(4,128)S(1)}, f32[4,4,128]{2,1,0:T(4,128)S(1)}, u32[]{:S(2)}, u32[]{:S(2)}) collective-permute-start(f32[4,4,128]{2,1,0:T(4,128)S(1)} %pad_maximum_fusion.70), channel_id=1, source_target_pairs={{0,32},{32,64},{64,96},{96,128},{128,160},{160,192},{192,224},{1,3... | collective-permute-start | bytes 24584 | tf_op jit(solution)/shard_map/while/body/eval_jaxpr/ppermute | solution.py:33
  255.9 1.8 copy-start.34
  274.4 1.0 copy-start.40
  274.4 1.0 copy-start.41
  289.6 2.0 copy-start.43
  295.1 1.0 copy-start.16
  300.3 4.8 %copy-start.33 = (f32[128,4,128]{2,0,1:T(8,128)S(1)}, f32[128,4,128]{2,0,1:T(8,128)}, u32[]{:S(2)}) copy-start(f32[128,4,128]{2,0,1:T(8,128)} %add.1036) | copy-start | bytes 786436
  305.3 2.6 copy-start.35
  307.9 1.0 copy-start.31
  309.0 2.6 copy-start.30
  311.8 24.7 %copy-start.44 = (f32[4,4,128]{2,1,0:T(4,128)S(1)}, f32[4,4,128]{2,1,0:T(4,128)}, u32[]{:S(2)}) copy-start(f32[4,4,128]{2,1,0:T(4,128)} %copy.75) | copy-start | bytes 24580
  311.8 138.9 %copy-start.21 = (f32[256,4,128]{2,0,1:T(8,128)S(1)}, f32[256,4,128]{2,0,1:T(8,128)}, u32[]{:S(2)}) copy-start(f32[256,4,128]{2,0,1:T(8,128)} %rev.17) | copy-start | bytes 1572868
  311.9 138.9 %copy-start.22 = (f32[256,4,128]{2,0,1:T(8,128)S(1)}, f32[256,4,128]{2,0,1:T(8,128)}, u32[]{:S(2)}) copy-start(f32[256,4,128]{2,0,1:T(8,128)} %rev.18) | copy-start | bytes 1572868
  314.5 136.3 %copy-start.20 = (f32[256,4,128]{2,0,1:T(8,128)S(1)}, f32[256,4,128]{2,0,1:T(8,128)}, u32[]{:S(2)}) copy-start(f32[256,4,128]{2,0,1:T(8,128)} %rev.16) | copy-start | bytes 1572868
  403.0 7.0 %collective-permute-start.1 = (f32[4,4,128]{2,1,0:T(4,128)S(1)}, f32[4,4,128]{2,1,0:T(4,128)S(1)}, u32[]{:S(2)}, u32[]{:S(2)}) collective-permute-start(f32[4,4,128]{2,1,0:T(4,128)S(1)} %pad_maximum_fusion.72), channel_id=1, source_target_pairs={{32,0},{64,32},{96,64},{128,96},{160,128},{192,160},{224,192},{33,... | collective-permute-start | bytes 24584 | tf_op jit(solution)/shard_map/while/body/eval_jaxpr/ppermute | solution.py:33
  410.1 6.8 %collective-permute-start.1 = (f32[4,4,128]{2,1,0:T(4,128)S(1)}, f32[4,4,128]{2,1,0:T(4,128)S(1)}, u32[]{:S(2)}, u32[]{:S(2)}) collective-permute-start(f32[4,4,128]{2,1,0:T(4,128)S(1)} %pad_maximum_fusion.72), channel_id=1, source_target_pairs={{32,0},{64,32},{96,64},{128,96},{160,128},{192,160},{224,192},{33,... | collective-permute-start | bytes 24584 | tf_op jit(solution)/shard_map/while/body/eval_jaxpr/ppermute | solution.py:33
  416.9 6.8 %collective-permute-start.1 = (f32[4,4,128]{2,1,0:T(4,128)S(1)}, f32[4,4,128]{2,1,0:T(4,128)S(1)}, u32[]{:S(2)}, u32[]{:S(2)}) collective-permute-start(f32[4,4,128]{2,1,0:T(4,128)S(1)} %pad_maximum_fusion.72), channel_id=1, source_target_pairs={{32,0},{64,32},{96,64},{128,96},{160,128},{192,160},{224,192},{33,... | collective-permute-start | bytes 24584 | tf_op jit(solution)/shard_map/while/body/eval_jaxpr/ppermute | solution.py:33
  423.6 6.8 %collective-permute-start.1 = (f32[4,4,128]{2,1,0:T(4,128)S(1)}, f32[4,4,128]{2,1,0:T(4,128)S(1)}, u32[]{:S(2)}, u32[]{:S(2)}) collective-permute-start(f32[4,4,128]{2,1,0:T(4,128)S(1)} %pad_maximum_fusion.72), channel_id=1, source_target_pairs={{32,0},{64,32},{96,64},{128,96},{160,128},{192,160},{224,192},{33,... | collective-permute-start | bytes 24584 | tf_op jit(solution)/shard_map/while/body/eval_jaxpr/ppermute | solution.py:33
  430.4 6.8 %collective-permute-start.1 = (f32[4,4,128]{2,1,0:T(4,128)S(1)}, f32[4,4,128]{2,1,0:T(4,128)S(1)}, u32[]{:S(2)}, u32[]{:S(2)}) collective-permute-start(f32[4,4,128]{2,1,0:T(4,128)S(1)} %pad_maximum_fusion.72), channel_id=1, source_target_pairs={{32,0},{64,32},{96,64},{128,96},{160,128},{192,160},{224,192},{33,... | collective-permute-start | bytes 24584 | tf_op jit(solution)/shard_map/while/body/eval_jaxpr/ppermute | solution.py:33
  437.2 6.8 %collective-permute-start.1 = (f32[4,4,128]{2,1,0:T(4,128)S(1)}, f32[4,4,128]{2,1,0:T(4,128)S(1)}, u32[]{:S(2)}, u32[]{:S(2)}) collective-permute-start(f32[4,4,128]{2,1,0:T(4,128)S(1)} %pad_maximum_fusion.72), channel_id=1, source_target_pairs={{32,0},{64,32},{96,64},{128,96},{160,128},{192,160},{224,192},{33,... | collective-permute-start | bytes 24584 | tf_op jit(solution)/shard_map/while/body/eval_jaxpr/ppermute | solution.py:33
  444.0 6.8 %collective-permute-start.1 = (f32[4,4,128]{2,1,0:T(4,128)S(1)}, f32[4,4,128]{2,1,0:T(4,128)S(1)}, u32[]{:S(2)}, u32[]{:S(2)}) collective-permute-start(f32[4,4,128]{2,1,0:T(4,128)S(1)} %pad_maximum_fusion.72), channel_id=1, source_target_pairs={{32,0},{64,32},{96,64},{128,96},{160,128},{192,160},{224,192},{33,... | collective-permute-start | bytes 24584 | tf_op jit(solution)/shard_map/while/body/eval_jaxpr/ppermute | solution.py:33
  450.8 1.4 copy-start.28
  452.2 1.2 copy-start.29
  453.4 3.2 copy-start.1
  (34 other events, 23.0 us)
where the time goes:
time: 460 us; the launch traced here: 457 us
  blocking collectives  180 us (39%)
  local copies, waits for them, and re-layouts  139 us (30%)
  starting transfers between devices  50.9 us (11%)
  waiting for transfers between devices  43.5 us (9%)
  other arithmetic  33.2 us (7%)
  matrix products  5.46 us (1%)
    psum x2, blocking collectives, broadcast(): return lax.psum(block, axis)  133 us
    ppermute x14, starting transfers between devices, shifted(): return lax.ppermute(block, axis, route)  50.9 us
    all_gather x2, blocking collectives, entering_2(): gathered = lax.all_gather(part, axis)  47.2 us
    ppermute x14, waiting for transfers between devices, shifted(): return lax.ppermute(block, axis, route)  43.5 us
    pad x56, local copies, waits for them, and re-layouts, on_device(): lax.associative_scan(compose, (growth_real, growth_imag, scaling * drive[...  32.8 us
    slice x119, local copies, waits for them, and re-layouts, on_device(): lax.associative_scan(compose, (back_real, back_imag, weight * mean_real,...  30.6 us
    slice x107, local copies, waits for them, and re-layouts, on_device(): lax.associative_scan(compose, (growth_real, growth_imag, scaling * drive[...  28.8 us
    unnamed x174, local copies, waits for them, and re-layouts  28.5 us
  transfers between devices with their start and end apart: 14, of which 14 were waited for; matrix products, arithmetic and copies ran while one was open for 0% of the time, Pallas kernels for 0%

commit v1 on v0

v1 whole, which is shorter than its diff:
```python
import math

import jax
import jax.numpy as jnp
from jax import lax
from jax.experimental import pallas as pl
from jax.experimental.pallas import tpu as pltpu
from jax.sharding import PartitionSpec as P

spike_multiplier = 0.7

VMEM = pltpu.VMEM
SMEM = pltpu.SMEM


def cmul(ar, ai, br, bi):
    return ar * br - ai * bi, ar * bi + ai * br


def factor_of(flag):
    return jnp.where(flag == 1, jnp.float32(spike_multiplier), jnp.float32(1.0))


def summary_kernel(flags_ref, last_ref, u_ref, par_ref, out_ref):
    steps = u_ref.shape[0]
    half = u_ref.shape[2] // 2
    lam_r, lam_i = par_ref[0], par_ref[1]
    bk_r, bk_i = par_ref[2], par_ref[3]
    w_plain, w_spike = par_ref[4], par_ref[5]
    zero = jnp.zeros_like(lam_r)
    one = jnp.ones_like(lam_r)

    def step(t, carry, final):
        mr, mi, ar, ai, pr, pi, qr, qi, hr, hi = carry
        flag = flags_ref[t]
        f = factor_of(flag)
        lr, li = f * lam_r, f * lam_i
        u = u_ref[t]
        mr, mi = lr * mr - li * mi + u[:, :half], lr * mi + li * mr + u[:, half:]
        ar, ai = cmul(lr, li, ar, ai)
        w = jnp.where(flag == 1, w_spike, w_plain)
        br, bi = f * bk_r, f * bk_i
        if final:
            last = last_ref[0] == 1
            w = jnp.where(last, one, w)
            br = jnp.where(last, zero, br)
            bi = jnp.where(last, zero, bi)
        wmr, wmi = w * mr, w * mi
        war, wai = w * ar, w * ai
        tr, ti = cmul(hr, hi, wmr, wmi)
        pr, pi = pr + tr, pi + ti
        tr, ti = cmul(hr, hi, war, wai)
        qr, qi = qr + tr, qi + ti
        hr, hi = cmul(br, bi, hr, hi)
        return (mr, mi, ar, ai, pr, pi, qr, qi, hr, hi)

    carry = (zero, zero, one, zero, zero, zero, zero, zero, one, zero)
    carry = lax.fori_loop(0, steps - 1, lambda t, c: step(t, c, False), carry, unroll=8)
    carry = step(steps - 1, carry, True)
    mr, mi, ar, ai, pr, pi, qr, qi, hr, hi = carry
    for idx, v in enumerate((ar, ai, mr, mi, hr, hi, pr, pi, qr, qi)):
        out_ref[idx] = v


def segment_kernel(me_ref, g_ref, tot_ref, mine_ref, al_r, al_i, be_r, be_i):
    count = g_ref.shape[0]
    me = me_ref[0]
    zero = jnp.zeros(g_ref.shape[2:], jnp.float32)
    one = jnp.ones_like(zero)

    ar, ai, br, bi = one, zero, zero, zero
    rec = [one, zero, zero, zero]
    for k in range(count):
        sel = me == k
        rec = [jnp.where(sel, v, r) for v, r in zip((ar, ai, br, bi), rec)]
        al_r[k], al_i[k], be_r[k], be_i[k] = ar, ai, br, bi
        Ar, Ai, Br, Bi = g_ref[k, 0], g_ref[k, 1], g_ref[k, 2], g_ref[k, 3]
        ar, ai = cmul(Ar, Ai, ar, ai)
        nr, ni = cmul(Ar, Ai, br, bi)
        br, bi = nr + Br, ni + Bi
    fwd_tot = (ar, ai, br, bi)
    fwd_me = rec

    gr, gi, pr, pi, kr, ki = one, zero, zero, zero, zero, zero
    rec = [one, zero, zero, zero, zero, zero]
    for k in reversed(range(count)):
        sel = me == k
        rec = [jnp.where(sel, v, r) for v, r in zip((gr, gi, pr, pi, kr, ki), rec)]
        Gr, Gi = g_ref[k, 4], g_ref[k, 5]
        Pr, Pi = g_ref[k, 6], g_ref[k, 7]
        Qr, Qi = g_ref[k, 8], g_ref[k, 9]
        xr, xi = cmul(Qr, Qi, be_r[k], be_i[k])
        yr, yi = cmul(Qr, Qi, al_r[k], al_i[k])
        gr, gi = cmul(Gr, Gi, gr, gi)
        nr, ni = cmul(Gr, Gi, pr, pi)
        pr, pi = nr + Pr + xr, ni + Pi + xi
        nr, ni = cmul(Gr, Gi, kr, ki)
        kr, ki = nr + yr, ni + yi
    bwd_tot = (gr, gi, pr, pi, kr, ki)
    bwd_me = rec
    for idx, v in enumerate(fwd_tot + bwd_tot):
        tot_ref[idx] = v
    for idx, v in enumerate(list(fwd_me) + list(bwd_me)):
        mine_ref[idx] = v


def final_kernel(flags_ref, last_ref, myseg_ref, tot_ref, mine_ref, prior_ref, u_ref, par_ref,
                 out_ref, m_r, m_i):
    steps = u_ref.shape[0]
    half = u_ref.shape[2] // 2
    segs = tot_ref.shape[0]
    myseg = myseg_ref[0]
    zero = jnp.zeros(par_ref.shape[1:], jnp.float32)
    one = jnp.ones_like(zero)

    cr, ci = prior_ref[0], prior_ref[1]
    c_in = []
    c_my = [zero, zero]
    for s in range(segs):
        c_in.append((cr, ci))
        sel = myseg == s
        c_my = [jnp.where(sel, cr, c_my[0]), jnp.where(sel, ci, c_my[1])]
        Ar, Ai, Br, Bi = tot_ref[s, 0], tot_ref[s, 1], tot_ref[s, 2], tot_ref[s, 3]
        nr, ni = cmul(Ar, Ai, cr, ci)
        cr, ci = nr + Br, ni + Bi
    er, ei = zero, zero
    e_my = [zero, zero]
    for s in reversed(range(segs)):
        sel = myseg == s
        e_my = [jnp.where(sel, er, e_my[0]), jnp.where(sel, ei, e_my[1])]
        Gr, Gi = tot_ref[s, 4], tot_ref[s, 5]
        Pr, Pi = tot_ref[s, 6], tot_ref[s, 7]
        Kr, Ki = tot_ref[s, 8], tot_ref[s, 9]
        nr, ni = cmul(Gr, Gi, er, ei)
        xr, xi = cmul(Kr, Ki, c_in[s][0], c_in[s][1])
        er, ei = nr + Pr + xr, ni + Pi + xi
    nr, ni = cmul(mine_ref[0], mine_ref[1], c_my[0], c_my[1])
    cr, ci = nr + mine_ref[2], ni + mine_ref[3]
    nr, ni = cmul(mine_ref[4], mine_ref[5], e_my[0], e_my[1])
    xr, xi = cmul(mine_ref[8], mine_ref[9], c_my[0], c_my[1])
    er, ei = nr + mine_ref[6] + xr, ni + mine_ref[7] + xi

    lam_r, lam_i = par_ref[0], par_ref[1]
    bk_r, bk_i = par_ref[2], par_ref[3]
    w_plain, w_spike = par_ref[4], par_ref[5]

    def fwd(t, carry):
        mr, mi = carry
        f = factor_of(flags_ref[t])
        lr, li = f * lam_r, f * lam_i
        u = u_ref[t]
        mr, mi = lr * mr - li * mi + u[:, :half], lr * mi + li * mr + u[:, half:]
        m_r[t] = mr
        m_i[t] = mi
        return (mr, mi)

    lax.fori_loop(0, steps, fwd, (cr, ci), unroll=8)

    def bwd_step(t, carry, final):
        sr, si = carry
        flag = flags_ref[t]
        f = factor_of(flag)
        w = jnp.where(flag == 1, w_spike, w_plain)
        br, bi = f * bk_r, f * bk_i
        if final:
            last = last_ref[0] == 1
            w = jnp.where(last, one, w)
            br = jnp.where(last, zero, br)
            bi = jnp.where(last, zero, bi)
        nr, ni = cmul(br, bi, sr, si)
        sr, si = nr + w * m_r[t], ni + w * m_i[t]
        out_ref[t, :, :half] = sr
        out_ref[t, :, half:] = si
        return (sr, si)

    carry = bwd_step(steps - 1, (er, ei), True)
    lax.fori_loop(0, steps - 1, lambda j, c: bwd_step(steps - 2 - j, c, False), carry, unroll=8)


def on_device(
    sampled_data,
    update_weights,
    eigenbasis_columns,
    measuring_operator,
    eigen_damping,
    backward_damping,
    rotation_angle,
    switch_flags,
    prior_expectation,
):
    highest = lax.Precision.HIGHEST
    steps = sampled_data.shape[2]
    seg_index = lax.axis_index("seg")
    blk_index = lax.axis_index("blk")
    last = ((seg_index == lax.axis_size("seg") - 1) & (blk_index == lax.axis_size("blk") - 1))
    last = last.astype(jnp.int32).reshape(1)
    flags = switch_flags.astype(jnp.int32)

    forward_rate = eigen_damping[0]
    backward_rate = backward_damping[0]
    angle = rotation_angle[0]
    magnitude = jnp.exp(-forward_rate)
    smooth_magnitude = jnp.exp(-backward_rate)
    both = forward_rate + backward_rate
    params = jnp.stack(
        [
            magnitude * jnp.cos(angle),
            magnitude * jnp.sin(angle),
            smooth_magnitude * jnp.cos(angle),
            -(smooth_magnitude * jnp.sin(angle)),
            -jnp.expm1(-both),
            -jnp.expm1(jnp.float32(2.0 * math.log(spike_multiplier)) - both),
        ]
    )
    scaling = jnp.sqrt(-jnp.expm1(-2.0 * forward_rate))
    scaling2 = jnp.concatenate([scaling, scaling], axis=1)
    drive = jnp.einsum("asm,amt->tas", update_weights, sampled_data, precision=highest)
    u = drive * scaling2[None]

    mode_shape = forward_rate.shape
    summary = pl.pallas_call(
        summary_kernel,
        out_shape=jax.ShapeDtypeStruct((10,) + mode_shape, jnp.float32),
        in_specs=[
            pl.BlockSpec(memory_space=SMEM),
            pl.BlockSpec(memory_space=SMEM),
            pl.BlockSpec(memory_space=VMEM),
            pl.BlockSpec(memory_space=VMEM),
        ],
        out_specs=pl.BlockSpec(memory_space=VMEM),
    )(flags, last, u, params)

    gathered = lax.all_gather(summary, "blk")
    count = gathered.shape[0]
    tot, mine = pl.pallas_call(
        segment_kernel,
        out_shape=(
            jax.ShapeDtypeStruct((10,) + mode_shape, jnp.float32),
            jax.ShapeDtypeStruct((10,) + mode_shape, jnp.float32),
        ),
        in_specs=[pl.BlockSpec(memory_space=SMEM), pl.BlockSpec(memory_space=VMEM)],
        out_specs=(pl.BlockSpec(memory_space=VMEM), pl.BlockSpec(memory_space=VMEM)),
        scratch_shapes=[pltpu.VMEM((count,) + mode_shape, jnp.float32) for _ in range(4)],
    )(blk_index.astype(jnp.int32).reshape(1), gathered)

    seg_tot = lax.all_gather(tot, "seg")
    stacked = pl.pallas_call(
        final_kernel,
        out_shape=jax.ShapeDtypeStruct(u.shape, jnp.float32),
        in_specs=[pl.BlockSpec(memory_space=SMEM)] * 3 + [pl.BlockSpec(memory_space=VMEM)] * 5,
        out_specs=pl.BlockSpec(memory_space=VMEM),
        scratch_shapes=[pltpu.VMEM((steps,) + mode_shape, jnp.float32) for _ in range(2)],
    )(flags, last, seg_index.astype(jnp.int32).reshape(1), seg_tot, mine, prior_expectation, u, params)

    states = jnp.einsum("ars,tas->art", eigenbasis_columns, stacked, precision=highest).astype(
        jnp.bfloat16
    )
    fitted = (
        sampled_data - jnp.einsum("ams,tas->amt", measuring_operator, stacked, precision=highest)
    ).astype(jnp.bfloat16)
    return (states, fitted)


def solution(mesh):
    placed = (
        P(None, None, ("seg", "blk")),
        P(),
        P(),
        P(),
        P(("seg", "blk"), None, None),
        P(("seg", "blk"), None, None),
        P(("seg", "blk"), None, None),
        P(("seg", "blk")),
        P(),
    )
    return jax.shard_map(
        on_device,
        mesh=mesh,
        in_specs=placed,
        out_specs=(P(None, None, ("seg", "blk")), P(None, None, ("seg", "blk"))),
        check_vma=False,
    )
```

time: 460 us -> 84 us (0.18)
  the two profiles are of different devices: /device:TPU:96 before, /device:TPU:2 now
where the time goes in v1:
time: 84 us; the launch traced here: 83.6 us
  blocking collectives  57.6 us (69%)
  Pallas kernels  10.4 us (12%)
  matrix products  8.29 us (10%)
  local copies, waits for them, and re-layouts  4.81 us (6%)
  other arithmetic  1.73 us (2%)
    all_gather x1, blocking collectives, on_device(): seg_tot = lax.all_gather(tot, 'seg')  30.6 us
    all_gather x1, blocking collectives, on_device(): gathered = lax.all_gather(summary, 'blk')  27.1 us
    pallas_call x1, Pallas kernels, on_device(): pl.pallas_call(final_kernel, out_shape=jax.ShapeDtypeStruct(u.shape, jnp....  4.62 us
    unnamed x15, local copies, waits for them, and re-layouts  3.99 us
    pallas_call x1, Pallas kernels, on_device(): pl.pallas_call(summary_kernel, out_shape=jax.ShapeDtypeStruct((10,) + mod...  3.8 us
    dot_general x1, matrix products, on_device(): jnp.einsum('asm,amt->tas', update_weights, sampled_data, precision=highest)  3.08 us
    dot_general x1, matrix products, on_device(): jnp.einsum('ams,tas->amt', measuring_operator, stacked, precision=highest)  2.77 us
    dot_general x1, matrix products, on_device(): jnp.einsum('ars,tas->art', eigenbasis_columns, stacked, precision=highest)  2.45 us

profile of v1, /device:TPU:2, one launch (start us, length us, event | category | flops | bytes accessed | tf_op | source)
XLA Modules:
  0.0 83.6 jit_solution(1426742639383714767)
XLA Ops:
  0.6 0.0 copy-start
  0.6 0.0 copy-start.4
  0.7 0.8 fusion.6
  1.5 0.0 copy-done.4
  1.5 0.0 copy-start.5
  1.5 0.7 copy-done.5
  2.2 0.0 copy-start.3
  2.3 0.0 copy-done
  2.3 3.1 %fusion.7 = f32[4,256,256]{2,1,0:T(8,128)S(1)} fusion(f32[4,256,256]{2,1,0:T(8,128)} %param.9, f32[4,256,256]{2,1,0:T(8,128)S(1)} %copy-done), kind=kOutput, calls=%fused_computation.20 | convolution fusion | flops 805306368 | bytes 3145728 | tf_op jit(solution)/shard_map/asm,amt->tas/dot_general | solution.py:217
  5.4 0.0 copy-done.3
  5.4 1.6 %fusion.3.u_ref = f32[256,4,256]{2,1,0:T(4,128)} fusion(f32[4,256,256]{2,1,0:T(8,128)S(1)} %fusion.7, f32[4,256]{1,0:T(4,128)S(1)} %pad_maximum_fusion), kind=kLoop, calls=%fused_computation.6 | loop fusion | flops 262144 | bytes 2101248 | tf_op jit(solution)/shard_map/mul | solution.py:218
  7.0 3.8 %shard_map.104 = f32[10,4,128]{2,1,0:T(4,128)} custom-call(s32[256]{0:T(256)} %flags_ref.3, s32[1]{0:T(128)} %bitcast.last_ref, f32[256,4,256]{2,1,0:T(4,128)} %fusion.3.u_ref, f32[6,4,128]{2,1,0:T(4,128)} %copy-done.3), custom_call_target="tpu_custom_call" | custom-call | tf_op jit(solution)/shard_map/pallas_call | solution.py:221
  10.8 27.1 %all-gather = f32[320,4,128]{2,1,0:T(4,128)} all-gather(f32[10,4,128]{2,1,0:T(4,128)} %shard_map.104), channel_id=2, replica_groups=mesh['seg'=8,'blk'=32] {'blk'}, dimensions={0}, use_global_device_ids=true | all-gather | bytes 675840 | tf_op jit(solution)/shard_map/all_gather | solution.py:233
  37.9 2.0 %shard_map.105 = (f32[10,4,128]{2,1,0:T(4,128)}, f32[10,4,128]{2,1,0:T(4,128)}) custom-call(s32[1]{0:T(128)} %bitcast.2.me_ref, f32[32,10,4,128]{3,2,1,0:T(4,128)} %bitcast.21), custom_call_target="tpu_custom_call" | custom-call | tf_op jit(solution)/shard_map/pallas_call | solution.py:235
  39.9 30.6 %all-gather.1 = f32[80,4,128]{2,1,0:T(4,128)} all-gather(f32[10,4,128]{2,1,0:T(4,128)} %get-tuple-element.4), channel_id=3, replica_groups=mesh['seg'=8,'blk'=32] {'seg'}, dimensions={0}, use_global_device_ids=true | all-gather | bytes 184320 | tf_op jit(solution)/shard_map/all_gather | solution.py:246
  70.4 0.0 copy-start.2
  70.4 4.6 %shard_map.106 = f32[256,4,256]{2,1,0:T(4,128)} custom-call(s32[256]{0:T(256)} %flags_ref.3, s32[1]{0:T(128)} %bitcast.last_ref, s32[1]{0:T(128)} %bitcast.1.myseg_ref, f32[8,10,4,128]{3,2,1,0:T(4,128)} %bitcast.22, f32[10,4,128]{2,1,0:T(4,128)} %get-tuple-element.5.mine_ref, f32[2,4,128]{2,1,0:T(4,128)} %prior_ref.1, f32[256,4,256]{2,1,0:T(4,128)} %fusion.3.u_ref, ...), custom_call_target="tpu_custom_call" | custom-call | tf_op jit(solution)/shard_map/pallas_call | solution.py:247
  75.0 0.0 copy-done.2
  75.0 0.0 copy-start.1
  75.0 1.3 %copy.22 = f32[4,256,256]{1,2,0:T(8,128)} copy(f32[4,256,256]{2,1,0:T(8,128)S(1)} %copy-done.2) | data formatting | bytes 2097152 | tf_op args[0]
  76.4 0.0 copy-done.1
  76.4 2.8 %fusion.1 = bf16[4,256,256]{1,2,0:T(8,128)(2,1)S(1)} fusion(f32[4,256,256]{1,2,0:T(8,128)} %copy.22, f32[4,256,256]{2,1,0:T(8,128)} %param.12, f32[256,4,256]{2,1,0:T(4,128)S(1)} %copy-done.1), kind=kOutput, calls=%fused_computation.2 | convolution fusion | flops 805830656 | bytes 3670016 | tf_op jit(solution)/shard_map/ams,tas->amt/dot_general | solution.py:259
  79.1 1.0 %copy.24 = bf16[4,256,256]{2,1,0:T(8,128)(2,1)} copy(bf16[4,256,256]{1,2,0:T(8,128)(2,1)S(1)} %fusion.1) | data formatting | bytes 1048576
  80.1 2.4 %fusion.2 = bf16[4,256,256]{1,2,0:T(8,128)(2,1)S(1)} fusion(f32[4,256,256]{2,1,0:T(8,128)} %param.11, f32[256,4,256]{2,1,0:T(4,128)S(1)} %copy-done.1), kind=kOutput, calls=%fused_computation.4 | convolution fusion | flops 805568512 | bytes 2621440 | tf_op jit(solution)/shard_map/ars,tas->art/dot_general | solution.py:255
  82.6 1.0 %copy.23 = bf16[4,256,256]{2,1,0:T(8,128)(2,1)} copy(bf16[4,256,256]{1,2,0:T(8,128)(2,1)S(1)} %fusion.2) | data formatting | bytes 1048576
  (7 shorter events, 0.1 us)
Async XLA Ops:
  0.6 1.6 %copy-start = (f32[4,256,256]{2,1,0:T(8,128)S(1)}, f32[4,256,256]{2,1,0:T(8,128)}, u32[]{:S(2)}) copy-start(f32[4,256,256]{2,1,0:T(8,128)} %param.10) | copy-start | bytes 3145732
  0.6 0.8 copy-start.4
  1.5 0.7 copy-start.5
  2.2 3.1 %copy-start.3 = (f32[6,4,128]{2,1,0:T(4,128)}, f32[6,4,128]{2,1,0:T(4,128)S(1)}, u32[]{:S(2)}) copy-start(f32[6,4,128]{2,1,0:T(4,128)S(1)} %get-tuple-element.10.par_ref) | copy-start | bytes 36868
  70.4 4.6 %copy-start.2 = (f32[4,256,256]{2,1,0:T(8,128)S(1)}, f32[4,256,256]{2,1,0:T(8,128)}, u32[]{:S(2)}) copy-start(f32[4,256,256]{2,1,0:T(8,128)} %param.9) | copy-start | bytes 3145732
  75.0 1.3 %copy-start.1 = (f32[256,4,256]{2,1,0:T(4,128)S(1)}, f32[256,4,256]{2,1,0:T(4,128)}, u32[]{:S(2)}) copy-start(f32[256,4,256]{2,1,0:T(4,128)} %shard_map.106) | copy-start | bytes 3145732

commit v2 on v1

--- a/solution.py
+++ b/solution.py
@@ -27,6 +27,7 @@
     lam_r, lam_i = par_ref[0], par_ref[1]
     bk_r, bk_i = par_ref[2], par_ref[3]
     w_plain, w_spike = par_ref[4], par_ref[5]
+    scale = par_ref[6]
     zero = jnp.zeros_like(lam_r)
     one = jnp.ones_like(lam_r)
 
@@ -36,7 +37,7 @@
         f = factor_of(flag)
         lr, li = f * lam_r, f * lam_i
         u = u_ref[t]
-        mr, mi = lr * mr - li * mi + u[:, :half], lr * mi + li * mr + u[:, half:]
+        mr, mi = lr * mr - li * mi + scale * u[:, :half], lr * mi + li * mr + scale * u[:, half:]
         ar, ai = cmul(lr, li, ar, ai)
         w = jnp.where(flag == 1, w_spike, w_plain)
         br, bi = f * bk_r, f * bk_i
@@ -143,13 +144,14 @@
     lam_r, lam_i = par_ref[0], par_ref[1]
     bk_r, bk_i = par_ref[2], par_ref[3]
     w_plain, w_spike = par_ref[4], par_ref[5]
+    scale = par_ref[6]
 
     def fwd(t, carry):
         mr, mi = carry
         f = factor_of(flags_ref[t])
         lr, li = f * lam_r, f * lam_i
         u = u_ref[t]
-        mr, mi = lr * mr - li * mi + u[:, :half], lr * mi + li * mr + u[:, half:]
+        mr, mi = lr * mr - li * mi + scale * u[:, :half], lr * mi + li * mr + scale * u[:, half:]
         m_r[t] = mr
         m_i[t] = mi
         return (mr, mi)
@@ -175,6 +177,12 @@
 
     carry = bwd_step(steps - 1, (er, ei), True)
     lax.fori_loop(0, steps - 1, lambda j, c: bwd_step(steps - 2 - j, c, False), carry, unroll=8)
+
+
+def gathered_over(block, axis):
+    count = lax.axis_size(axis)
+    spread = jnp.broadcast_to(block[None], (count,) + block.shape)
+    return lax.all_to_all(spread, axis, 0, 0, tiled=False)
 
 
 def on_device(
@@ -213,9 +221,8 @@
         ]
     )
     scaling = jnp.sqrt(-jnp.expm1(-2.0 * forward_rate))
-    scaling2 = jnp.concatenate([scaling, scaling], axis=1)
-    drive = jnp.einsum("asm,amt->tas", update_weights, sampled_data, precision=highest)
-    u = drive * scaling2[None]
+    u = jnp.einsum("asm,amt->tas", update_weights, sampled_data, precision=highest)
+    params = jnp.concatenate([params, scaling[None]], axis=0)
 
     mode_shape = forward_rate.shape
     summary = pl.pallas_call(
@@ -230,7 +237,7 @@
         out_specs=pl.BlockSpec(memory_space=VMEM),
     )(flags, last, u, params)
 
-    gathered = lax.all_gather(summary, "blk")
+    gathered = gathered_over(summary, "blk")
     count = gathered.shape[0]
     tot, mine = pl.pallas_call(
         segment_kernel,
@@ -243,7 +250,7 @@
         scratch_shapes=[pltpu.VMEM((count,) + mode_shape, jnp.float32) for _ in range(4)],
     )(blk_index.astype(jnp.int32).reshape(1), gathered)
 
-    seg_tot = lax.all_gather(tot, "seg")
+    seg_tot = gathered_over(tot, "seg")
     stacked = pl.pallas_call(
         final_kernel,
         out_shape=jax.ShapeDtypeStruct(u.shape, jnp.float32),

time: 84 us -> 69.7 us (0.83)
  the two profiles are of different devices: /device:TPU:2 before, /device:TPU:1 now
where the time goes in v2:
time: 69.7 us; the launch traced here: 69.1 us
  blocking collectives  21.5 us (31%)
  Pallas kernels  10.4 us (15%)
  waiting for transfers between devices  9.82 us (14%)
  local copies, waits for them, and re-layouts  9.51 us (14%)
  matrix products  8.77 us (13%)
  starting transfers between devices  8.19 us (12%)
  between operations  0.77 us (1%)
    all_to_all x1, blocking collectives, gathered_over(): return lax.all_to_all(spread, axis, 0, 0, tiled=False)  21.5 us
    all_to_all x1, waiting for transfers between devices, gathered_over(): return lax.all_to_all(spread, axis, 0, 0, tiled=False)  9.82 us
    all_to_all x1, starting transfers between devices, gathered_over(): return lax.all_to_all(spread, axis, 0, 0, tiled=False)  8.19 us
    unnamed x19, local copies, waits for them, and re-layouts  4.82 us
    pallas_call x1, Pallas kernels, on_device(): pl.pallas_call(final_kernel, out_shape=jax.ShapeDtypeStruct(u.shape, jnp....  4.61 us
    pallas_call x1, Pallas kernels, on_device(): pl.pallas_call(summary_kernel, out_shape=jax.ShapeDtypeStruct((10,) + mod...  3.8 us
    dot_general x1, matrix products, on_device(): jnp.einsum('ams,tas->amt', measuring_operator, stacked, precision=highest)  3.24 us
    dot_general x1, matrix products, on_device(): jnp.einsum('asm,amt->tas', update_weights, sampled_data, precision=highest)  3.08 us
  transfers between devices with their start and end apart: 1, of which 1 were waited for; matrix products, arithmetic and copies ran while one was open for 0% of the time, Pallas kernels for 0%

profile of v2, /device:TPU:1, one launch (start us, length us, event | category | flops | bytes accessed | tf_op | source)
XLA Modules:
  0.0 69.1 jit_solution(6857982467757895711)
XLA Ops:
  0.6 0.0 copy-start
  0.6 0.0 copy-start.6
  0.7 0.8 %fusion.5 = (f32[1,4,128]{2,1,0:T(4,128)S(1)}, f32[1,4,128]{2,1,0:T(4,128)S(1)}) fusion(f32[1,4,128]{2,1,0:T(4,128)} %param.15), kind=kLoop, calls=%fused_computation.17 | loop fusion | bytes 6144 | tf_op jit(solution)/shard_map/sin | solution.py:216
  1.5 0.0 copy-done.6
  1.5 0.0 copy-start.7
  1.5 0.7 copy-done.7
  2.3 0.0 copy-start.5
  2.3 0.0 copy-done
  2.3 3.1 %fusion.6 = f32[4,256,256]{2,1,0:T(8,128)S(1)} fusion(f32[4,256,256]{2,1,0:T(8,128)} %param.9, f32[4,256,256]{2,1,0:T(8,128)S(1)} %copy-done), kind=kOutput, calls=%fused_computation.18 | convolution fusion | flops 805306368 | bytes 3145728 | tf_op jit(solution)/shard_map/asm,amt->tas/dot_general | solution.py:224
  5.4 0.0 copy-done.5
  5.4 1.6 %copy.24 = f32[4,256,256]{2,0,1:T(4,128)} copy(f32[4,256,256]{2,1,0:T(8,128)S(1)} %fusion.6) | data formatting | bytes 2097152 | tf_op jit(solution)/shard_map/asm,amt->tas/dot_general | solution.py:224
  7.0 3.8 %shard_map.104 = f32[10,4,128]{2,1,0:T(4,128)} custom-call(s32[256]{0:T(256)} %flags_ref.3, s32[1]{0:T(128)} %bitcast.last_ref, f32[256,4,256]{2,1,0:T(4,128)} %bitcast.18, f32[7,4,128]{2,1,0:T(4,128)} %copy-done.5), custom_call_target="tpu_custom_call" | custom-call | tf_op jit(solution)/shard_map/pallas_call | solution.py:228
  10.8 0.8 %broadcast_in_dim.4 = f32[32,10,4,128]{3,2,1,0:T(4,128)S(1)} broadcast(f32[10,4,128]{2,1,0:T(4,128)} %shard_map.104), dimensions={1,2,3} | broadcast | bytes 675840 | tf_op jit(solution)/shard_map/broadcast_in_dim | solution.py:184
  11.7 0.0 copy-start.2
  11.7 21.5 %all_to_all.10.g_ref = f32[32,10,4,128]{3,2,1,0:T(4,128)} all-to-all(f32[32,10,4,128]{3,2,1,0:T(4,128)S(1)} %broadcast_in_dim.4), channel_id=1, replica_groups=mesh['seg'=8,'blk'=32] {'blk'}, dimensions={0} | all-to-all | bytes 1310720 | tf_op jit(solution)/shard_map/all_to_all | solution.py:185
  33.2 2.0 %shard_map.105 = (f32[10,4,128]{2,1,0:T(4,128)}, f32[10,4,128]{2,1,0:T(4,128)}) custom-call(s32[1]{0:T(128)} %bitcast.2.me_ref, f32[32,10,4,128]{3,2,1,0:T(4,128)} %all_to_all.10.g_ref), custom_call_target="tpu_custom_call" | custom-call | tf_op jit(solution)/shard_map/pallas_call | solution.py:242
  35.2 1.4 %broadcast_in_dim.5 = f32[8,10,4,128]{3,2,1,0:T(4,128)} broadcast(f32[10,4,128]{2,1,0:T(4,128)} %get-tuple-element.4), dimensions={1,2,3} | broadcast | bytes 184320 | tf_op jit(solution)/shard_map/broadcast_in_dim | solution.py:184
  36.6 8.2 %all-to-all-start.1 = ((f32[8,10,4,128]{3,2,1,0:T(4,128)}), f32[8,10,4,128]{3,2,1,0:T(4,128)S(1)}, u32[]{:S(2)}, u32[]{:S(2)}) async-start(f32[8,10,4,128]{3,2,1,0:T(4,128)} %broadcast_in_dim.5), calls=%async_computation.1 | async-start | bytes 327680 | tf_op jit(solution)/shard_map/all_to_all | solution.py:185
  44.8 0.0 copy-done.2
  44.8 0.3 copy.15
  45.1 9.8 %all-to-all-done.1.tot_ref = f32[8,10,4,128]{3,2,1,0:T(4,128)S(1)} async-done(((f32[8,10,4,128]{3,2,1,0:T(4,128)}), f32[8,10,4,128]{3,2,1,0:T(4,128)S(1)}, u32[]{:S(2)}, u32[]{:S(2)}) %all-to-all-start.1) | async-done | bytes 163872 | tf_op jit(solution)/shard_map/all_to_all | solution.py:185
  55.0 0.0 copy-start.4
  55.0 0.7 copy-done.4
  55.6 0.0 copy-start.3
  55.6 4.6 %shard_map.106 = f32[256,4,256]{2,1,0:T(4,128)} custom-call(s32[256]{0:T(256)} %flags_ref.3, s32[1]{0:T(128)} %bitcast.last_ref, s32[1]{0:T(128)} %bitcast.1.myseg_ref, f32[8,10,4,128]{3,2,1,0:T(4,128)} %copy-done.4, f32[10,4,128]{2,1,0:T(4,128)} %get-tuple-element.5.mine_ref, f32[2,4,128]{2,1,0:T(4,128)} %prior_ref.1, f32[256,4,256]{2,1,0:T(4,128)} %bitcast.19, ...), custom_call_target="tpu_custom_call" | custom-call | tf_op jit(solution)/shard_map/pallas_call | solution.py:254
  60.2 0.0 copy-done.3
  60.2 3.2 %fusion.1 = bf16[4,256,256]{1,2,0:T(8,128)(2,1)} fusion(f32[4,256,256]{1,2,0:T(8,128)S(1)} %copy.15, f32[4,256,256]{2,1,0:T(8,128)S(1)} %copy-done.3, f32[256,4,256]{2,1,0:T(4,128)} %shard_map.106), kind=kOutput, calls=%fused_computation.2 | convolution fusion | flops 805830656 | bytes 3670016 | tf_op jit(solution)/shard_map/ams,tas->amt/dot_general | solution.py:266
  63.5 0.0 copy-start.1
  63.5 2.1 %copy.17 = bf16[4,256,256]{2,1,0:T(8,128)(2,1)} copy(bf16[4,256,256]{1,2,0:T(8,128)(2,1)} %fusion.1) | data formatting | bytes 1048576
  65.6 0.0 copy-done.1
  65.6 2.4 %fusion.2 = bf16[4,256,256]{1,2,0:T(8,128)(2,1)S(1)} fusion(f32[4,256,256]{2,1,0:T(8,128)} %param.11, f32[256,4,256]{2,1,0:T(4,128)S(1)} %copy-done.1), kind=kOutput, calls=%fused_computation.4 | convolution fusion | flops 805568512 | bytes 2621440 | tf_op jit(solution)/shard_map/ars,tas->art/dot_general | solution.py:262
  68.1 1.0 %copy.16 = bf16[4,256,256]{2,1,0:T(8,128)(2,1)} copy(bf16[4,256,256]{1,2,0:T(8,128)(2,1)S(1)} %fusion.2) | data formatting | bytes 1048576
  (7 shorter events, 0.1 us)
Async XLA Ops:
  0.6 1.7 %copy-start = (f32[4,256,256]{2,1,0:T(8,128)S(1)}, f32[4,256,256]{2,1,0:T(8,128)}, u32[]{:S(2)}) copy-start(f32[4,256,256]{2,1,0:T(8,128)} %param.10) | copy-start | bytes 3145732
  0.6 0.8 %copy-start.6 = (f32[1,4,128]{2,1,0:T(4,128)S(1)}, f32[1,4,128]{2,1,0:T(4,128)}, u32[]{:S(2)}) copy-start(f32[1,4,128]{2,1,0:T(4,128)} %param.13) | copy-start | bytes 6148
  1.5 0.7 copy-start.7
  2.3 3.1 %copy-start.5 = (f32[7,4,128]{2,1,0:T(4,128)}, f32[7,4,128]{2,1,0:T(4,128)S(1)}, u32[]{:S(2)}) copy-start(f32[7,4,128]{2,1,0:T(4,128)S(1)} %constant_dynamic-update-slice_fusion.par_ref) | copy-start | bytes 43012
  11.7 33.1 %copy-start.2 = (f32[4,256,256]{2,1,0:T(8,128)S(1)}, f32[4,256,256]{2,1,0:T(8,128)}, u32[]{:S(2)}) copy-start(f32[4,256,256]{2,1,0:T(8,128)} %param.9) | copy-start | bytes 3145732
  36.6 18.4 %all-to-all-start.1 = ((f32[8,10,4,128]{3,2,1,0:T(4,128)}), f32[8,10,4,128]{3,2,1,0:T(4,128)S(1)}, u32[]{:S(2)}, u32[]{:S(2)}) async-start(f32[8,10,4,128]{3,2,1,0:T(4,128)} %broadcast_in_dim.5), calls=%async_computation.1 | async-start | bytes 327680 | tf_op jit(solution)/shard_map/all_to_all | solution.py:185
  55.0 0.7 copy-start.4
  55.6 4.6 %copy-start.3 = (f32[4,256,256]{2,1,0:T(8,128)S(1)}, f32[4,256,256]{2,1,0:T(8,128)}, u32[]{:S(2)}) copy-start(f32[4,256,256]{2,1,0:T(8,128)} %param.12) | copy-start | bytes 3145732
  63.5 2.1 %copy-start.1 = (f32[256,4,256]{2,1,0:T(4,128)S(1)}, f32[256,4,256]{2,1,0:T(4,128)}, u32[]{:S(2)}) copy-start(f32[256,4,256]{2,1,0:T(4,128)} %shard_map.106) | copy-start | bytes 3145732

commit v3 on v2

--- a/solution.py
+++ b/solution.py
@@ -60,7 +60,8 @@
     carry = step(steps - 1, carry, True)
     mr, mi, ar, ai, pr, pi, qr, qi, hr, hi = carry
     for idx, v in enumerate((ar, ai, mr, mi, hr, hi, pr, pi, qr, qi)):
-        out_ref[idx] = v
+        for k in range(out_ref.shape[0]):
+            out_ref[k, idx] = v
 
 
 def segment_kernel(me_ref, g_ref, tot_ref, mine_ref, al_r, al_i, be_r, be_i):
@@ -100,7 +101,8 @@
     bwd_tot = (gr, gi, pr, pi, kr, ki)
     bwd_me = rec
     for idx, v in enumerate(fwd_tot + bwd_tot):
-        tot_ref[idx] = v
+        for s in range(tot_ref.shape[0]):
+            tot_ref[s, idx] = v
     for idx, v in enumerate(list(fwd_me) + list(bwd_me)):
         mine_ref[idx] = v
 
@@ -179,9 +181,7 @@
     lax.fori_loop(0, steps - 1, lambda j, c: bwd_step(steps - 2 - j, c, False), carry, unroll=8)
 
 
-def gathered_over(block, axis):
-    count = lax.axis_size(axis)
-    spread = jnp.broadcast_to(block[None], (count,) + block.shape)
+def gathered_over(spread, axis):
     return lax.all_to_all(spread, axis, 0, 0, tiled=False)
 
 
@@ -196,7 +196,7 @@
     switch_flags,
     prior_expectation,
 ):
-    highest = lax.Precision.HIGHEST
+    highest = lax.Precision.HIGH
     steps = sampled_data.shape[2]
     seg_index = lax.axis_index("seg")
     blk_index = lax.axis_index("blk")
@@ -227,7 +227,7 @@
     mode_shape = forward_rate.shape
     summary = pl.pallas_call(
         summary_kernel,
-        out_shape=jax.ShapeDtypeStruct((10,) + mode_shape, jnp.float32),
+        out_shape=jax.ShapeDtypeStruct((lax.axis_size("blk"), 10) + mode_shape, jnp.float32),
         in_specs=[
             pl.BlockSpec(memory_space=SMEM),
             pl.BlockSpec(memory_space=SMEM),
@@ -242,7 +242,7 @@
     tot, mine = pl.pallas_call(
         segment_kernel,
         out_shape=(
-            jax.ShapeDtypeStruct((10,) + mode_shape, jnp.float32),
+            jax.ShapeDtypeStruct((lax.axis_size("seg"), 10) + mode_shape, jnp.float32),
             jax.ShapeDtypeStruct((10,) + mode_shape, jnp.float32),
         ),
         in_specs=[pl.BlockSpec(memory_space=SMEM), pl.BlockSpec(memory_space=VMEM)],

time: 69.7 us -> 66.2 us (0.950)
  local copies, waits for them, and re-layouts: 9.51 us -> 7.28 us
  matrix products: 8.77 us -> 7.03 us
    broadcast_in_dim x2 -> x0, local copies, waits for them, and re-layouts: 2.23 us -> none  [gathered_over(): spread = jnp.broadcast_to(block[None], (count,) + block.shape)]
    dot_general x1, matrix products: 3.08 us -> 2.27 us  [on_device(): jnp.einsum('asm,amt->tas', update_weights, sampled_data, precision=highest)]
  transfers between devices with their start and end apart: 1 -> 1, of which waited for: 1 -> 1; matrix products, arithmetic and copies ran while one was open for 0% -> 1% of each run, Pallas kernels for 0% -> 0%
where the time goes in v3:
time: 66.2 us; the launch traced here: 65.7 us
  blocking collectives  21.7 us (33%)
  Pallas kernels  10.8 us (16%)
  waiting for transfers between devices  9.82 us (15%)
  starting transfers between devices  8.18 us (12%)
  local copies, waits for them, and re-layouts  7.28 us (11%)
  matrix products  7.03 us (11%)
  between operations  0.76 us (1%)
    all_to_all x1, blocking collectives, gathered_over(): return lax.all_to_all(spread, axis, 0, 0, tiled=False)  21.7 us
    all_to_all x1, waiting for transfers between devices, gathered_over(): return lax.all_to_all(spread, axis, 0, 0, tiled=False)  9.82 us
    all_to_all x1, starting transfers between devices, gathered_over(): return lax.all_to_all(spread, axis, 0, 0, tiled=False)  8.18 us
    unnamed x19, local copies, waits for them, and re-layouts  4.82 us
    pallas_call x1, Pallas kernels, on_device(): pl.pallas_call(final_kernel, out_shape=jax.ShapeDtypeStruct(u.shape, jnp....  4.61 us
    pallas_call x1, Pallas kernels, on_device(): pl.pallas_call(summary_kernel, out_shape=jax.ShapeDtypeStruct((lax.axis_s...  4.1 us
    dot_general x1, matrix products, on_device(): jnp.einsum('ams,tas->amt', measuring_operator, stacked, precision=highest)  2.79 us
    dot_general x1, matrix products, on_device(): jnp.einsum('asm,amt->tas', update_weights, sampled_data, precision=highest)  2.27 us
  transfers between devices with their start and end apart: 1, of which 1 were waited for; matrix products, arithmetic and copies ran while one was open for 1% of the time, Pallas kernels for 0%

profile of v3, /device:TPU:1, one launch (start us, length us, event | category | flops | bytes accessed | tf_op | source)
XLA Modules:
  0.0 65.7 jit_solution(18034494750725052589)
XLA Ops:
  0.6 0.0 copy-start
  0.6 0.0 copy-start.6
  0.7 0.8 %fusion.5 = (f32[1,4,128]{2,1,0:T(4,128)S(1)}, f32[1,4,128]{2,1,0:T(4,128)S(1)}) fusion(f32[1,4,128]{2,1,0:T(4,128)} %param.15), kind=kLoop, calls=%fused_computation.17 | loop fusion | bytes 6144 | tf_op jit(solution)/shard_map/sin | solution.py:216
  1.5 0.0 copy-done.6
  1.5 0.0 copy-start.7
  1.5 0.7 %copy-done.7 = f32[1,4,128]{2,1,0:T(4,128)S(1)} copy-done((f32[1,4,128]{2,1,0:T(4,128)S(1)}, f32[1,4,128]{2,1,0:T(4,128)}, u32[]{:S(2)}) %copy-start.7) | copy-done | bytes 2072
  2.3 0.0 copy-start.5
  2.3 0.0 copy-done
  2.3 2.3 %fusion.6 = f32[4,256,256]{2,1,0:T(8,128)S(1)} fusion(f32[4,256,256]{2,1,0:T(8,128)} %param.9, f32[4,256,256]{2,1,0:T(8,128)S(1)} %copy-done), kind=kOutput, calls=%fused_computation.18 | convolution fusion | flops 402653184 | bytes 3145728 | tf_op jit(solution)/shard_map/asm,amt->tas/dot_general | solution.py:224
  4.6 0.0 copy-done.5
  4.6 1.6 %copy.24 = f32[4,256,256]{2,0,1:T(4,128)} copy(f32[4,256,256]{2,1,0:T(8,128)S(1)} %fusion.6) | data formatting | bytes 2097152 | tf_op jit(solution)/shard_map/asm,amt->tas/dot_general | solution.py:224
  6.2 4.1 %shard_map.104 = f32[32,10,4,128]{3,2,1,0:T(4,128)} custom-call(s32[256]{0:T(256)} %flags_ref.3, s32[1]{0:T(128)} %bitcast.last_ref, f32[256,4,256]{2,1,0:T(4,128)} %bitcast.18, f32[7,4,128]{2,1,0:T(4,128)} %copy-done.5), custom_call_target="tpu_custom_call" | custom-call | tf_op jit(solution)/shard_map/pallas_call | solution.py:228
  10.3 0.0 copy-start.2
  10.3 21.7 %all_to_all.10.g_ref = f32[32,10,4,128]{3,2,1,0:T(4,128)} all-to-all(f32[32,10,4,128]{3,2,1,0:T(4,128)} %shard_map.104), channel_id=1, replica_groups=mesh['seg'=8,'blk'=32] {'blk'}, dimensions={0} | all-to-all | bytes 1310720 | tf_op jit(solution)/shard_map/all_to_all | solution.py:185
  32.1 2.1 %shard_map.105 = (f32[8,10,4,128]{3,2,1,0:T(4,128)}, f32[10,4,128]{2,1,0:T(4,128)}) custom-call(s32[1]{0:T(128)} %bitcast.2.me_ref, f32[32,10,4,128]{3,2,1,0:T(4,128)} %all_to_all.10.g_ref), custom_call_target="tpu_custom_call" | custom-call | tf_op jit(solution)/shard_map/pallas_call | solution.py:242
  34.1 8.2 %all-to-all-start.1 = ((f32[8,10,4,128]{3,2,1,0:T(4,128)}), f32[8,10,4,128]{3,2,1,0:T(4,128)S(1)}, u32[]{:S(2)}, u32[]{:S(2)}) async-start(f32[8,10,4,128]{3,2,1,0:T(4,128)} %get-tuple-element.4), calls=%async_computation.1 | async-start | bytes 327680 | tf_op jit(solution)/shard_map/all_to_all | solution.py:185
  42.3 0.0 copy-done.2
  42.3 0.3 copy.15
  42.7 9.8 %all-to-all-done.1.tot_ref = f32[8,10,4,128]{3,2,1,0:T(4,128)S(1)} async-done(((f32[8,10,4,128]{3,2,1,0:T(4,128)}), f32[8,10,4,128]{3,2,1,0:T(4,128)S(1)}, u32[]{:S(2)}, u32[]{:S(2)}) %all-to-all-start.1) | async-done | bytes 163872 | tf_op jit(solution)/shard_map/all_to_all | solution.py:185
  52.5 0.0 copy-start.4
  52.5 0.7 %copy-done.4 = f32[8,10,4,128]{3,2,1,0:T(4,128)} copy-done((f32[8,10,4,128]{3,2,1,0:T(4,128)}, f32[8,10,4,128]{3,2,1,0:T(4,128)S(1)}, u32[]{:S(2)}) %copy-start.4) | copy-done | bytes 163864
  53.1 0.0 copy-start.3
  53.1 4.6 %shard_map.106 = f32[256,4,256]{2,1,0:T(4,128)} custom-call(s32[256]{0:T(256)} %flags_ref.3, s32[1]{0:T(128)} %bitcast.last_ref, s32[1]{0:T(128)} %bitcast.1.myseg_ref, f32[8,10,4,128]{3,2,1,0:T(4,128)} %copy-done.4, f32[10,4,128]{2,1,0:T(4,128)} %get-tuple-element.5.mine_ref, f32[2,4,128]{2,1,0:T(4,128)} %prior_ref.1, f32[256,4,256]{2,1,0:T(4,128)} %bitcast.19, ...), custom_call_target="tpu_custom_call" | custom-call | tf_op jit(solution)/shard_map/pallas_call | solution.py:254
  57.8 0.0 copy-done.3
  57.8 2.8 %fusion.1 = bf16[4,256,256]{1,2,0:T(8,128)(2,1)} fusion(f32[4,256,256]{1,2,0:T(8,128)S(1)} %copy.15, f32[4,256,256]{2,1,0:T(8,128)S(1)} %copy-done.3, f32[256,4,256]{2,1,0:T(4,128)} %shard_map.106), kind=kOutput, calls=%fused_computation.2 | convolution fusion | flops 403177472 | bytes 3670016 | tf_op jit(solution)/shard_map/ams,tas->amt/dot_general | solution.py:266
  60.6 0.0 copy-start.1
  60.6 2.1 %copy.17 = bf16[4,256,256]{2,1,0:T(8,128)(2,1)} copy(bf16[4,256,256]{1,2,0:T(8,128)(2,1)} %fusion.1) | data formatting | bytes 1048576
  62.7 0.0 copy-done.1
  62.7 2.0 %fusion.2 = bf16[4,256,256]{1,2,0:T(8,128)(2,1)S(1)} fusion(f32[4,256,256]{2,1,0:T(8,128)} %param.11, f32[256,4,256]{2,1,0:T(4,128)S(1)} %copy-done.1), kind=kOutput, calls=%fused_computation.4 | convolution fusion | flops 402915328 | bytes 2621440 | tf_op jit(solution)/shard_map/ars,tas->art/dot_general | solution.py:262
  64.7 1.0 %copy.16 = bf16[4,256,256]{2,1,0:T(8,128)(2,1)} copy(bf16[4,256,256]{1,2,0:T(8,128)(2,1)S(1)} %fusion.2) | data formatting | bytes 1048576
  (7 shorter events, 0.1 us)
Async XLA Ops:
  0.6 1.7 %copy-start = (f32[4,256,256]{2,1,0:T(8,128)S(1)}, f32[4,256,256]{2,1,0:T(8,128)}, u32[]{:S(2)}) copy-start(f32[4,256,256]{2,1,0:T(8,128)} %param.10) | copy-start | bytes 3145732
  0.6 0.8 %copy-start.6 = (f32[1,4,128]{2,1,0:T(4,128)S(1)}, f32[1,4,128]{2,1,0:T(4,128)}, u32[]{:S(2)}) copy-start(f32[1,4,128]{2,1,0:T(4,128)} %param.13) | copy-start | bytes 6148
  1.5 0.7 %copy-start.7 = (f32[1,4,128]{2,1,0:T(4,128)S(1)}, f32[1,4,128]{2,1,0:T(4,128)}, u32[]{:S(2)}) copy-start(f32[1,4,128]{2,1,0:T(4,128)} %param.14) | copy-start | bytes 6148
  2.3 2.3 %copy-start.5 = (f32[7,4,128]{2,1,0:T(4,128)}, f32[7,4,128]{2,1,0:T(4,128)S(1)}, u32[]{:S(2)}) copy-start(f32[7,4,128]{2,1,0:T(4,128)S(1)} %constant_dynamic-update-slice_fusion.par_ref) | copy-start | bytes 43012
  10.3 32.0 %copy-start.2 = (f32[4,256,256]{2,1,0:T(8,128)S(1)}, f32[4,256,256]{2,1,0:T(8,128)}, u32[]{:S(2)}) copy-start(f32[4,256,256]{2,1,0:T(8,128)} %param.9) | copy-start | bytes 3145732
  34.1 18.4 %all-to-all-start.1 = ((f32[8,10,4,128]{3,2,1,0:T(4,128)}), f32[8,10,4,128]{3,2,1,0:T(4,128)S(1)}, u32[]{:S(2)}, u32[]{:S(2)}) async-start(f32[8,10,4,128]{3,2,1,0:T(4,128)} %get-tuple-element.4), calls=%async_computation.1 | async-start | bytes 327680 | tf_op jit(solution)/shard_map/all_to_all | solution.py:185
  52.5 0.7 %copy-start.4 = (f32[8,10,4,128]{3,2,1,0:T(4,128)}, f32[8,10,4,128]{3,2,1,0:T(4,128)S(1)}, u32[]{:S(2)}) copy-start(f32[8,10,4,128]{3,2,1,0:T(4,128)S(1)} %all-to-all-done.1.tot_ref) | copy-start | bytes 491524
  53.1 4.6 %copy-start.3 = (f32[4,256,256]{2,1,0:T(8,128)S(1)}, f32[4,256,256]{2,1,0:T(8,128)}, u32[]{:S(2)}) copy-start(f32[4,256,256]{2,1,0:T(8,128)} %param.12) | copy-start | bytes 3145732
  60.6 2.1 %copy-start.1 = (f32[256,4,256]{2,1,0:T(4,128)S(1)}, f32[256,4,256]{2,1,0:T(4,128)}, u32[]{:S(2)}) copy-start(f32[256,4,256]{2,1,0:T(4,128)} %shard_map.106) | copy-start | bytes 3145732

commit v4 on v3

--- a/solution.py
+++ b/solution.py
@@ -21,7 +21,15 @@
     return jnp.where(flag == 1, jnp.float32(spike_multiplier), jnp.float32(1.0))
 
 
-def summary_kernel(flags_ref, last_ref, u_ref, par_ref, out_ref):
+def fill_drive(w_ref, d_ref, u_ref):
+    for a in range(w_ref.shape[0]):
+        u_ref[:, a, :] = lax.dot_general(
+            d_ref[a], w_ref[a], (((0,), (1,)), ((), ())),
+            precision=lax.Precision.HIGHEST, preferred_element_type=jnp.float32)
+
+
+def summary_kernel(flags_ref, last_ref, w_ref, d_ref, par_ref, out_ref, u_ref):
+    fill_drive(w_ref, d_ref, u_ref)
     steps = u_ref.shape[0]
     half = u_ref.shape[2] // 2
     lam_r, lam_i = par_ref[0], par_ref[1]
@@ -107,8 +115,9 @@
         mine_ref[idx] = v
 
 
-def final_kernel(flags_ref, last_ref, myseg_ref, tot_ref, mine_ref, prior_ref, u_ref, par_ref,
-                 out_ref, m_r, m_i):
+def final_kernel(flags_ref, last_ref, myseg_ref, tot_ref, mine_ref, prior_ref, w_ref, d_ref, e_ref,
+                 o_ref, par_ref, states_ref, fitted_ref, u_ref, m_r, m_i, out_ref):
+    fill_drive(w_ref, d_ref, u_ref)
     steps = u_ref.shape[0]
     half = u_ref.shape[2] // 2
     segs = tot_ref.shape[0]
@@ -180,6 +189,16 @@
     carry = bwd_step(steps - 1, (er, ei), True)
     lax.fori_loop(0, steps - 1, lambda j, c: bwd_step(steps - 2 - j, c, False), carry, unroll=8)
 
+    contract = (((1,), (1,)), ((), ()))
+    for a in range(e_ref.shape[0]):
+        stacked = out_ref[:, a, :]
+        states = lax.dot_general(e_ref[a], stacked, contract, precision=lax.Precision.HIGHEST,
+                                 preferred_element_type=jnp.float32)
+        states_ref[a] = states.astype(states_ref.dtype)
+        seen = lax.dot_general(o_ref[a], stacked, contract, precision=lax.Precision.HIGHEST,
+                               preferred_element_type=jnp.float32)
+        fitted_ref[a] = (d_ref[a] - seen).astype(fitted_ref.dtype)
+
 
 def gathered_over(spread, axis):
     return lax.all_to_all(spread, axis, 0, 0, tiled=False)
@@ -196,7 +215,6 @@
     switch_flags,
     prior_expectation,
 ):
-    highest = lax.Precision.HIGH
     steps = sampled_data.shape[2]
     seg_index = lax.axis_index("seg")
     blk_index = lax.axis_index("blk")
@@ -221,21 +239,17 @@
         ]
     )
     scaling = jnp.sqrt(-jnp.expm1(-2.0 * forward_rate))
-    u = jnp.einsum("asm,amt->tas", update_weights, sampled_data, precision=highest)
     params = jnp.concatenate([params, scaling[None]], axis=0)
+    u_shape = (steps, sampled_data.shape[0], sampled_data.shape[1])
 
     mode_shape = forward_rate.shape
     summary = pl.pallas_call(
         summary_kernel,
         out_shape=jax.ShapeDtypeStruct((lax.axis_size("blk"), 10) + mode_shape, jnp.float32),
-        in_specs=[
-            pl.BlockSpec(memory_space=SMEM),
-            pl.BlockSpec(memory_space=SMEM),
-            pl.BlockSpec(memory_space=VMEM),
-            pl.BlockSpec(memory_space=VMEM),
-        ],
+        in_specs=[pl.BlockSpec(memory_space=SMEM)] * 2 + [pl.BlockSpec(memory_space=VMEM)] * 3,
         out_specs=pl.BlockSpec(memory_space=VMEM),
-    )(flags, last, u, params)
+        scratch_shapes=[pltpu.VMEM(u_shape, jnp.float32)],
+    )(flags, last, update_weights, sampled_data, params)
 
     gathered = gathered_over(summary, "blk")
     count = gathered.shape[0]
@@ -251,20 +265,17 @@
     )(blk_index.astype(jnp.int32).reshape(1), gathered)
 
     seg_tot = gathered_over(tot, "seg")
-    stacked = pl.pallas_call(
+    out_block = jax.ShapeDtypeStruct(sampled_data.shape, jnp.bfloat16)
+    states, fitted = pl.pallas_call(
         final_kernel,
-        out_shape=jax.ShapeDtypeStruct(u.shape, jnp.float32),
-        in_specs=[pl.BlockSpec(memory_space=SMEM)] * 3 + [pl.BlockSpec(memory_space=VMEM)] * 5,
-        out_specs=pl.BlockSpec(memory_space=VMEM),
-        scratch_shapes=[pltpu.VMEM((steps,) + mode_shape, jnp.float32) for _ in range(2)],
-    )(flags, last, seg_index.astype(jnp.int32).reshape(1), seg_tot, mine, prior_expectation, u, params)
-
-    states = jnp.einsum("ars,tas->art", eigenbasis_columns, stacked, precision=highest).astype(
-        jnp.bfloat16
-    )
-    fitted = (
-        sampled_data - jnp.einsum("ams,tas->amt", measuring_operator, stacked, precision=highest)
-    ).astype(jnp.bfloat16)
+        out_shape=(out_block, out_block),
+        in_specs=[pl.BlockSpec(memory_space=SMEM)] * 3 + [pl.BlockSpec(memory_space=VMEM)] * 8,
+        out_specs=(pl.BlockSpec(memory_space=VMEM), pl.BlockSpec(memory_space=VMEM)),
+        scratch_shapes=[pltpu.VMEM(u_shape, jnp.float32)]
+        + [pltpu.VMEM((steps,) + mode_shape, jnp.float32) for _ in range(2)]
+        + [pltpu.VMEM(u_shape, jnp.float32)],
+    )(flags, last, seg_index.astype(jnp.int32).reshape(1), seg_tot, mine, prior_expectation,
+      update_weights, sampled_data, eigenbasis_columns, measuring_operator, params)
     return (states, fitted)
 
 

time: 66.2 us -> 60.7 us (0.917)
  blocking collectives: 21.7 us -> 40 us
  waiting for transfers between devices: 9.82 us -> 0 us
  starting transfers between devices: 8.18 us -> 0 us
  matrix products: 7.03 us -> 0 us
  Pallas kernels: 10.8 us -> 16.9 us
  local copies, waits for them, and re-layouts: 7.28 us -> 2.63 us
    all_to_all x1 -> x2, blocking collectives: 21.7 us -> 40 us  [gathered_over(): return lax.all_to_all(spread, axis, 0, 0, tiled=False)]
    all_to_all x1 -> x0, waiting for transfers between devices: 9.82 us -> none  [gathered_over(): return lax.all_to_all(spread, axis, 0, 0, tiled=False)]
    all_to_all x1 -> x0, starting transfers between devices: 8.18 us -> none  [gathered_over(): return lax.all_to_all(spread, axis, 0, 0, tiled=False)]
    dot_general x3 -> x0, matrix products: 7.03 us -> none  [the longest x1 2.79 us: on_device(): jnp.einsum('ams,tas->amt', measuring_operator, stacked, precision=highest)]
    pallas_call x1, Pallas kernels: 4.61 us -> 8.99 us  [on_device(): pl.pallas_call(final_kernel, out_shape=(out_block, out_block), in_specs=[...]
    unnamed x19 -> x8, local copies, waits for them, and re-layouts: 4.82 us -> 2.59 us
    pallas_call x1, Pallas kernels: 4.1 us -> 5.81 us  [on_device(): pl.pallas_call(summary_kernel, out_shape=jax.ShapeDtypeStruct((lax.axis_s...]
    dot_general x1 -> x0, local copies, waits for them, and re-layouts: 1.65 us -> none  [on_device(): jnp.einsum('asm,amt->tas', update_weights, sampled_data, precision=highest)]
  transfers between devices with their start and end apart: 1 -> 0, of which waited for: 1 -> 0; matrix products, arithmetic and copies ran while one was open for 1% -> 0% of each run, Pallas kernels for 0% -> 0%
where the time goes in v4:
time: 60.7 us; the launch traced here: 60.3 us
  blocking collectives  40 us (66%)
  Pallas kernels  16.9 us (28%)
  local copies, waits for them, and re-layouts  2.63 us (4%)
  between operations  0.68 us (1%)
    all_to_all x2, blocking collectives, gathered_over(): return lax.all_to_all(spread, axis, 0, 0, tiled=False)  40 us
    pallas_call x1, Pallas kernels, on_device(): pl.pallas_call(final_kernel, out_shape=(out_block, out_block), in_specs=[...  8.99 us
    pallas_call x1, Pallas kernels, on_device(): pl.pallas_call(summary_kernel, out_shape=jax.ShapeDtypeStruct((lax.axis_s...  5.81 us
    unnamed x8, local copies, waits for them, and re-layouts  2.59 us
    pallas_call x1, Pallas kernels, on_device(): pl.pallas_call(segment_kernel, out_shape=(jax.ShapeDtypeStruct((lax.axis_...  2.06 us

profile of v4, /device:TPU:1, one launch (start us, length us, event | category | flops | bytes accessed | tf_op | source)
XLA Modules:
  0.0 60.3 jit_solution(8963994314856197852)
XLA Ops:
  0.6 0.0 copy-start.3
  0.7 0.7 %copy-done.3 = f32[1,4,128]{2,1,0:T(4,128)S(1)} copy-done((f32[1,4,128]{2,1,0:T(4,128)S(1)}, f32[1,4,128]{2,1,0:T(4,128)}, u32[]{:S(2)}) %copy-start.3) | copy-done | bytes 2072
  1.3 0.0 copy-start.1
  1.4 0.6 %copy-done.1 = f32[1,4,128]{2,1,0:T(4,128)S(1)} copy-done((f32[1,4,128]{2,1,0:T(4,128)S(1)}, f32[1,4,128]{2,1,0:T(4,128)}, u32[]{:S(2)}) %copy-start.1) | copy-done | bytes 2072
  2.0 0.0 copy-start.2
  2.0 0.7 %copy-done.2 = f32[1,4,128]{2,1,0:T(4,128)S(1)} copy-done((f32[1,4,128]{2,1,0:T(4,128)S(1)}, f32[1,4,128]{2,1,0:T(4,128)}, u32[]{:S(2)}) %copy-start.2) | copy-done | bytes 2072
  2.8 0.0 copy-start
  2.8 0.6 copy-done
  3.4 5.8 %shard_map.104 = f32[32,10,4,128]{3,2,1,0:T(4,128)} custom-call(s32[256]{0:T(256)} %flags_ref.3, s32[1]{0:T(128)} %bitcast.last_ref, f32[4,256,256]{2,1,0:T(8,128)} %w_ref.3, f32[4,256,256]{2,1,0:T(8,128)} %d_ref.3, f32[7,4,128]{2,1,0:T(4,128)} %copy-done), custom_call_target="tpu_custom_call" | custom-call | tf_op jit(solution)/shard_map/pallas_call | solution.py:246
  9.2 21.6 %all_to_all.10.g_ref = f32[32,10,4,128]{3,2,1,0:T(4,128)} all-to-all(f32[32,10,4,128]{3,2,1,0:T(4,128)} %shard_map.104), channel_id=1, replica_groups=mesh['seg'=8,'blk'=32] {'blk'}, dimensions={0} | all-to-all | bytes 1310720 | tf_op jit(solution)/shard_map/all_to_all | solution.py:204
  30.8 2.1 %shard_map.105 = (f32[8,10,4,128]{3,2,1,0:T(4,128)}, f32[10,4,128]{2,1,0:T(4,128)}) custom-call(s32[1]{0:T(128)} %bitcast.2.me_ref, f32[32,10,4,128]{3,2,1,0:T(4,128)} %all_to_all.10.g_ref), custom_call_target="tpu_custom_call" | custom-call | tf_op jit(solution)/shard_map/pallas_call | solution.py:256
  32.9 18.5 %all_to_all.11.tot_ref = f32[8,10,4,128]{3,2,1,0:T(4,128)} all-to-all(f32[8,10,4,128]{3,2,1,0:T(4,128)} %get-tuple-element.4), channel_id=1, replica_groups=mesh['seg'=8,'blk'=32] {'seg'}, dimensions={0} | all-to-all | bytes 327680 | tf_op jit(solution)/shard_map/all_to_all | solution.py:204
  51.3 9.0 %shard_map.106 = (bf16[4,256,256]{2,1,0:T(8,128)(2,1)}, bf16[4,256,256]{2,1,0:T(8,128)(2,1)}) custom-call(s32[256]{0:T(256)} %flags_ref.3, s32[1]{0:T(128)} %bitcast.last_ref, s32[1]{0:T(128)} %bitcast.1.myseg_ref, f32[8,10,4,128]{3,2,1,0:T(4,128)} %all_to_all.11.tot_ref, f32[10,4,128]{2,1,0:T(4,128)} %get-tuple-element.5.mine_ref, f32[2,4,128]{2,1,0:T(4,128)} %prior_ref.1, ...), custom_call_target="tpu_custom_call" | custom-call | tf_op jit(solution)/shard_map/pallas_call | solution.py:269
  (8 shorter events, 0.1 us)
Async XLA Ops:
  0.6 0.7 %copy-start.3 = (f32[1,4,128]{2,1,0:T(4,128)S(1)}, f32[1,4,128]{2,1,0:T(4,128)}, u32[]{:S(2)}) copy-start(f32[1,4,128]{2,1,0:T(4,128)} %param.15) | copy-start | bytes 6148
  1.3 0.7 %copy-start.1 = (f32[1,4,128]{2,1,0:T(4,128)S(1)}, f32[1,4,128]{2,1,0:T(4,128)}, u32[]{:S(2)}) copy-start(f32[1,4,128]{2,1,0:T(4,128)} %param.13) | copy-start | bytes 6148
  2.0 0.7 %copy-start.2 = (f32[1,4,128]{2,1,0:T(4,128)S(1)}, f32[1,4,128]{2,1,0:T(4,128)}, u32[]{:S(2)}) copy-start(f32[1,4,128]{2,1,0:T(4,128)} %param.14) | copy-start | bytes 6148
  2.8 0.6 %copy-start = (f32[7,4,128]{2,1,0:T(4,128)}, f32[7,4,128]{2,1,0:T(4,128)S(1)}, u32[]{:S(2)}) copy-start(f32[7,4,128]{2,1,0:T(4,128)S(1)} %constant_dynamic-update-slice_fusion.par_ref) | copy-start | bytes 43012

commit v5 on v4

--- a/solution.py
+++ b/solution.py
@@ -21,11 +21,25 @@
     return jnp.where(flag == 1, jnp.float32(spike_multiplier), jnp.float32(1.0))
 
 
+def split_bf16(x):
+    high = x.astype(jnp.bfloat16)
+    low = (x - high.astype(jnp.float32)).astype(jnp.bfloat16)
+    return high, low
+
+
+def dot3(x, y, dims):
+    xh, xl = split_bf16(x)
+    yh, yl = split_bf16(y)
+
+    def one(p, q):
+        return lax.dot_general(p, q, dims, preferred_element_type=jnp.float32)
+
+    return one(xh, yh) + (one(xh, yl) + one(xl, yh))
+
+
 def fill_drive(w_ref, d_ref, u_ref):
     for a in range(w_ref.shape[0]):
-        u_ref[:, a, :] = lax.dot_general(
-            d_ref[a], w_ref[a], (((0,), (1,)), ((), ())),
-            precision=lax.Precision.HIGHEST, preferred_element_type=jnp.float32)
+        u_ref[:, a, :] = dot3(d_ref[a], w_ref[a], (((0,), (1,)), ((), ())))
 
 
 def summary_kernel(flags_ref, last_ref, w_ref, d_ref, par_ref, out_ref, u_ref):
@@ -115,8 +129,12 @@
         mine_ref[idx] = v
 
 
-def final_kernel(flags_ref, last_ref, myseg_ref, tot_ref, mine_ref, prior_ref, w_ref, d_ref, e_ref,
-                 o_ref, par_ref, states_ref, fitted_ref, u_ref, m_r, m_i, out_ref):
+def final_kernel(flags_ref, last_ref, myseg_ref, tot_ref, mine_ref, prior_ref, w_ref, d_ref, e_hbm,
+                 o_hbm, par_ref, states_ref, fitted_ref, u_ref, m_r, m_i, out_ref, e_ref, o_ref, sems):
+    e_copy = pltpu.make_async_copy(e_hbm, e_ref, sems.at[0])
+    o_copy = pltpu.make_async_copy(o_hbm, o_ref, sems.at[1])
+    e_copy.start()
+    o_copy.start()
     fill_drive(w_ref, d_ref, u_ref)
     steps = u_ref.shape[0]
     half = u_ref.shape[2] // 2
@@ -189,14 +207,14 @@
     carry = bwd_step(steps - 1, (er, ei), True)
     lax.fori_loop(0, steps - 1, lambda j, c: bwd_step(steps - 2 - j, c, False), carry, unroll=8)
 
+    e_copy.wait()
+    o_copy.wait()
     contract = (((1,), (1,)), ((), ()))
     for a in range(e_ref.shape[0]):
         stacked = out_ref[:, a, :]
-        states = lax.dot_general(e_ref[a], stacked, contract, precision=lax.Precision.HIGHEST,
-                                 preferred_element_type=jnp.float32)
+        states = dot3(e_ref[a], stacked, contract)
         states_ref[a] = states.astype(states_ref.dtype)
-        seen = lax.dot_general(o_ref[a], stacked, contract, precision=lax.Precision.HIGHEST,
-                               preferred_element_type=jnp.float32)
+        seen = dot3(o_ref[a], stacked, contract)
         fitted_ref[a] = (d_ref[a] - seen).astype(fitted_ref.dtype)
 
 
@@ -269,11 +287,14 @@
     states, fitted = pl.pallas_call(
         final_kernel,
         out_shape=(out_block, out_block),
-        in_specs=[pl.BlockSpec(memory_space=SMEM)] * 3 + [pl.BlockSpec(memory_space=VMEM)] * 8,
+        in_specs=[pl.BlockSpec(memory_space=SMEM)] * 3 + [pl.BlockSpec(memory_space=VMEM)] * 5
+        + [pl.BlockSpec(memory_space=pl.ANY)] * 2 + [pl.BlockSpec(memory_space=VMEM)],
         out_specs=(pl.BlockSpec(memory_space=VMEM), pl.BlockSpec(memory_space=VMEM)),
         scratch_shapes=[pltpu.VMEM(u_shape, jnp.float32)]
         + [pltpu.VMEM((steps,) + mode_shape, jnp.float32) for _ in range(2)]
-        + [pltpu.VMEM(u_shape, jnp.float32)],
+        + [pltpu.VMEM(u_shape, jnp.float32)]
+        + [pltpu.VMEM(eigenbasis_columns.shape, jnp.float32) for _ in range(2)]
+        + [pltpu.SemaphoreType.DMA((2,))],
     )(flags, last, seg_index.astype(jnp.int32).reshape(1), seg_tot, mine, prior_expectation,
       update_weights, sampled_data, eigenbasis_columns, measuring_operator, params)
     return (states, fitted)

time: 60.7 us -> 60.6 us (level)
    pallas_call x1, Pallas kernels: 5.81 us -> 5.17 us  [on_device(): pl.pallas_call(summary_kernel, out_shape=jax.ShapeDtypeStruct((lax.axis_s...]
where the time goes in v5:
time: 60.6 us; the launch traced here: 60.2 us
  blocking collectives  40 us (66%)
  Pallas kernels  16.7 us (28%)
  local copies, waits for them, and re-layouts  2.63 us (4%)
  between operations  0.68 us (1%)
    all_to_all x2, blocking collectives, gathered_over(): return lax.all_to_all(spread, axis, 0, 0, tiled=False)  40 us
    pallas_call x1, Pallas kernels, on_device(): pl.pallas_call(final_kernel, out_shape=(out_block, out_block), in_specs=[...  9.51 us
    pallas_call x1, Pallas kernels, on_device(): pl.pallas_call(summary_kernel, out_shape=jax.ShapeDtypeStruct((lax.axis_s...  5.17 us
    unnamed x8, local copies, waits for them, and re-layouts  2.59 us
    pallas_call x1, Pallas kernels, on_device(): pl.pallas_call(segment_kernel, out_shape=(jax.ShapeDtypeStruct((lax.axis_...  2.06 us

profile of v5, /device:TPU:1, one launch (start us, length us, event | category | flops | bytes accessed | tf_op | source)
XLA Modules:
  0.0 60.2 jit_solution(6294090595019436159)
XLA Ops:
  0.6 0.0 copy-start.3
  0.7 0.7 %copy-done.3 = f32[1,4,128]{2,1,0:T(4,128)S(1)} copy-done((f32[1,4,128]{2,1,0:T(4,128)S(1)}, f32[1,4,128]{2,1,0:T(4,128)}, u32[]{:S(2)}) %copy-start.3) | copy-done | bytes 2072
  1.3 0.0 copy-start.1
  1.4 0.6 %copy-done.1 = f32[1,4,128]{2,1,0:T(4,128)S(1)} copy-done((f32[1,4,128]{2,1,0:T(4,128)S(1)}, f32[1,4,128]{2,1,0:T(4,128)}, u32[]{:S(2)}) %copy-start.1) | copy-done | bytes 2072
  2.0 0.0 copy-start.2
  2.0 0.7 %copy-done.2 = f32[1,4,128]{2,1,0:T(4,128)S(1)} copy-done((f32[1,4,128]{2,1,0:T(4,128)S(1)}, f32[1,4,128]{2,1,0:T(4,128)}, u32[]{:S(2)}) %copy-start.2) | copy-done | bytes 2072
  2.8 0.0 copy-start
  2.8 0.6 copy-done
  3.4 5.2 %shard_map.104 = f32[32,10,4,128]{3,2,1,0:T(4,128)} custom-call(s32[256]{0:T(256)} %flags_ref.3, s32[1]{0:T(128)} %bitcast.last_ref, f32[4,256,256]{2,1,0:T(8,128)} %w_ref.3, f32[4,256,256]{2,1,0:T(8,128)} %d_ref.3, f32[7,4,128]{2,1,0:T(4,128)} %copy-done), custom_call_target="tpu_custom_call" | custom-call | tf_op jit(solution)/shard_map/pallas_call | solution.py:264
  8.6 21.6 %all_to_all.10.g_ref = f32[32,10,4,128]{3,2,1,0:T(4,128)} all-to-all(f32[32,10,4,128]{3,2,1,0:T(4,128)} %shard_map.104), channel_id=1, replica_groups=mesh['seg'=8,'blk'=32] {'blk'}, dimensions={0} | all-to-all | bytes 1310720 | tf_op jit(solution)/shard_map/all_to_all | solution.py:222
  30.2 2.1 %shard_map.105 = (f32[8,10,4,128]{3,2,1,0:T(4,128)}, f32[10,4,128]{2,1,0:T(4,128)}) custom-call(s32[1]{0:T(128)} %bitcast.2.me_ref, f32[32,10,4,128]{3,2,1,0:T(4,128)} %all_to_all.10.g_ref), custom_call_target="tpu_custom_call" | custom-call | tf_op jit(solution)/shard_map/pallas_call | solution.py:274
  32.2 18.5 %all_to_all.11.tot_ref = f32[8,10,4,128]{3,2,1,0:T(4,128)} all-to-all(f32[8,10,4,128]{3,2,1,0:T(4,128)} %get-tuple-element.4), channel_id=1, replica_groups=mesh['seg'=8,'blk'=32] {'seg'}, dimensions={0} | all-to-all | bytes 327680 | tf_op jit(solution)/shard_map/all_to_all | solution.py:222
  50.7 9.5 %shard_map.106 = (bf16[4,256,256]{2,1,0:T(8,128)(2,1)}, bf16[4,256,256]{2,1,0:T(8,128)(2,1)}) custom-call(s32[256]{0:T(256)} %flags_ref.3, s32[1]{0:T(128)} %bitcast.last_ref, s32[1]{0:T(128)} %bitcast.1.myseg_ref, f32[8,10,4,128]{3,2,1,0:T(4,128)} %all_to_all.11.tot_ref, f32[10,4,128]{2,1,0:T(4,128)} %get-tuple-element.5.mine_ref, f32[2,4,128]{2,1,0:T(4,128)} %prior_ref.1, ...), custom_call_target="tpu_custom_call" | custom-call | tf_op jit(solution)/shard_map/pallas_call | solution.py:287
  (8 shorter events, 0.1 us)
Async XLA Ops:
  0.6 0.7 %copy-start.3 = (f32[1,4,128]{2,1,0:T(4,128)S(1)}, f32[1,4,128]{2,1,0:T(4,128)}, u32[]{:S(2)}) copy-start(f32[1,4,128]{2,1,0:T(4,128)} %param.15) | copy-start | bytes 6148
  1.3 0.7 %copy-start.1 = (f32[1,4,128]{2,1,0:T(4,128)S(1)}, f32[1,4,128]{2,1,0:T(4,128)}, u32[]{:S(2)}) copy-start(f32[1,4,128]{2,1,0:T(4,128)} %param.13) | copy-start | bytes 6148
  2.0 0.7 %copy-start.2 = (f32[1,4,128]{2,1,0:T(4,128)S(1)}, f32[1,4,128]{2,1,0:T(4,128)}, u32[]{:S(2)}) copy-start(f32[1,4,128]{2,1,0:T(4,128)} %param.14) | copy-start | bytes 6148
  2.8 0.6 %copy-start = (f32[7,4,128]{2,1,0:T(4,128)}, f32[7,4,128]{2,1,0:T(4,128)S(1)}, u32[]{:S(2)}) copy-start(f32[7,4,128]{2,1,0:T(4,128)S(1)} %constant_dynamic-update-slice_fusion.par_ref) | copy-start | bytes 43012

commit v6 on v5

--- a/solution.py
+++ b/solution.py
@@ -21,6 +21,41 @@
     return jnp.where(flag == 1, jnp.float32(spike_multiplier), jnp.float32(1.0))
 
 
+LOG_SPIKE_TWICE = 2.0 * math.log(spike_multiplier)
+
+
+def expm1(x):
+    small = jnp.abs(x) < 0.5
+    xs = jnp.where(small, x, 0.0)
+    p = jnp.ones_like(x)
+    for k in range(12, 1, -1):
+        p = 1.0 + (xs * jnp.float32(1.0 / k)) * p
+    return jnp.where(small, xs * p, jnp.exp(x) - 1.0)
+
+
+def mode_params(fd, bd, th):
+    mag = jnp.exp(-fd)
+    smag = jnp.exp(-bd)
+    cos, sin = jnp.cos(th), jnp.sin(th)
+    both = fd + bd
+    return (
+        mag * cos,
+        mag * sin,
+        smag * cos,
+        -(smag * sin),
+        -expm1(-both),
+        -expm1(jnp.float32(LOG_SPIKE_TWICE) - both),
+        jnp.sqrt(-expm1(-2.0 * fd)),
+    )
+
+
+def start_rate_copies(rate_hbm, rate_ref, sems, first):
+    copies = [pltpu.make_async_copy(rate_hbm[i], rate_ref.at[i], sems.at[first + i]) for i in range(3)]
+    for c in copies:
+        c.start()
+    return copies
+
+
 def split_bf16(x):
     high = x.astype(jnp.bfloat16)
     low = (x - high.astype(jnp.float32)).astype(jnp.bfloat16)
@@ -42,14 +77,16 @@
         u_ref[:, a, :] = dot3(d_ref[a], w_ref[a], (((0,), (1,)), ((), ())))
 
 
-def summary_kernel(flags_ref, last_ref, w_ref, d_ref, par_ref, out_ref, u_ref):
+def summary_kernel(flags_ref, last_ref, w_ref, d_ref, fd_hbm, bd_hbm, th_hbm, out_ref, u_ref,
+                   rate_ref, sems):
+    copies = start_rate_copies((fd_hbm, bd_hbm, th_hbm), rate_ref, sems, 0)
     fill_drive(w_ref, d_ref, u_ref)
+    for c in copies:
+        c.wait()
     steps = u_ref.shape[0]
     half = u_ref.shape[2] // 2
-    lam_r, lam_i = par_ref[0], par_ref[1]
-    bk_r, bk_i = par_ref[2], par_ref[3]
-    w_plain, w_spike = par_ref[4], par_ref[5]
-    scale = par_ref[6]
+    lam_r, lam_i, bk_r, bk_i, w_plain, w_spike, scale = mode_params(
+        rate_ref[0, 0], rate_ref[1, 0], rate_ref[2, 0])
     zero = jnp.zeros_like(lam_r)
     one = jnp.ones_like(lam_r)
 
@@ -130,17 +167,19 @@
 
 
 def final_kernel(flags_ref, last_ref, myseg_ref, tot_ref, mine_ref, prior_ref, w_ref, d_ref, e_hbm,
-                 o_hbm, par_ref, states_ref, fitted_ref, u_ref, m_r, m_i, out_ref, e_ref, o_ref, sems):
+                 o_hbm, fd_hbm, bd_hbm, th_hbm, states_ref, fitted_ref, u_ref, m_r, m_i, out_ref, e_ref,
+                 o_ref, rate_ref, sems):
     e_copy = pltpu.make_async_copy(e_hbm, e_ref, sems.at[0])
     o_copy = pltpu.make_async_copy(o_hbm, o_ref, sems.at[1])
     e_copy.start()
     o_copy.start()
+    copies = start_rate_copies((fd_hbm, bd_hbm, th_hbm), rate_ref, sems, 2)
     fill_drive(w_ref, d_ref, u_ref)
     steps = u_ref.shape[0]
     half = u_ref.shape[2] // 2
     segs = tot_ref.shape[0]
     myseg = myseg_ref[0]
-    zero = jnp.zeros(par_ref.shape[1:], jnp.float32)
+    zero = jnp.zeros(prior_ref.shape[1:], jnp.float32)
     one = jnp.ones_like(zero)
 
     cr, ci = prior_ref[0], prior_ref[1]
@@ -170,10 +209,10 @@
     xr, xi = cmul(mine_ref[8], mine_ref[9], c_my[0], c_my[1])
     er, ei = nr + mine_ref[6] + xr, ni + mine_ref[7] + xi
 
-    lam_r, lam_i = par_ref[0], par_ref[1]
-    bk_r, bk_i = par_ref[2], par_ref[3]
-    w_plain, w_spike = par_ref[4], par_ref[5]
-    scale = par_ref[6]
+    for c in copies:
+        c.wait()
+    lam_r, lam_i, bk_r, bk_i, w_plain, w_spike, scale = mode_params(
+        rate_ref[0, 0], rate_ref[1, 0], rate_ref[2, 0])
 
     def fwd(t, carry):
         mr, mi = carry
@@ -240,34 +279,19 @@
     last = last.astype(jnp.int32).reshape(1)
     flags = switch_flags.astype(jnp.int32)
 
-    forward_rate = eigen_damping[0]
-    backward_rate = backward_damping[0]
-    angle = rotation_angle[0]
-    magnitude = jnp.exp(-forward_rate)
-    smooth_magnitude = jnp.exp(-backward_rate)
-    both = forward_rate + backward_rate
-    params = jnp.stack(
-        [
-            magnitude * jnp.cos(angle),
-            magnitude * jnp.sin(angle),
-            smooth_magnitude * jnp.cos(angle),
-            -(smooth_magnitude * jnp.sin(angle)),
-            -jnp.expm1(-both),
-            -jnp.expm1(jnp.float32(2.0 * math.log(spike_multiplier)) - both),
-        ]
-    )
-    scaling = jnp.sqrt(-jnp.expm1(-2.0 * forward_rate))
-    params = jnp.concatenate([params, scaling[None]], axis=0)
     u_shape = (steps, sampled_data.shape[0], sampled_data.shape[1])
-
-    mode_shape = forward_rate.shape
+    rates = (eigen_damping, backward_damping, rotation_angle)
+    rate_scratch = pltpu.VMEM((3,) + eigen_damping.shape, jnp.float32)
+
+    mode_shape = eigen_damping.shape[1:]
     summary = pl.pallas_call(
         summary_kernel,
         out_shape=jax.ShapeDtypeStruct((lax.axis_size("blk"), 10) + mode_shape, jnp.float32),
-        in_specs=[pl.BlockSpec(memory_space=SMEM)] * 2 + [pl.BlockSpec(memory_space=VMEM)] * 3,
+        in_specs=[pl.BlockSpec(memory_space=SMEM)] * 2 + [pl.BlockSpec(memory_space=VMEM)] * 2
+        + [pl.BlockSpec(memory_space=pl.ANY)] * 3,
         out_specs=pl.BlockSpec(memory_space=VMEM),
-        scratch_shapes=[pltpu.VMEM(u_shape, jnp.float32)],
-    )(flags, last, update_weights, sampled_data, params)
+        scratch_shapes=[pltpu.VMEM(u_shape, jnp.float32), rate_scratch, pltpu.SemaphoreType.DMA((3,))],
+    )(flags, last, update_weights, sampled_data, *rates)
 
     gathered = gathered_over(summary, "blk")
     count = gathered.shape[0]
@@ -288,15 +312,15 @@
         final_kernel,
         out_shape=(out_block, out_block),
         in_specs=[pl.BlockSpec(memory_space=SMEM)] * 3 + [pl.BlockSpec(memory_space=VMEM)] * 5
-        + [pl.BlockSpec(memory_space=pl.ANY)] * 2 + [pl.BlockSpec(memory_space=VMEM)],
+        + [pl.BlockSpec(memory_space=pl.ANY)] * 5,
         out_specs=(pl.BlockSpec(memory_space=VMEM), pl.BlockSpec(memory_space=VMEM)),
         scratch_shapes=[pltpu.VMEM(u_shape, jnp.float32)]
         + [pltpu.VMEM((steps,) + mode_shape, jnp.float32) for _ in range(2)]
         + [pltpu.VMEM(u_shape, jnp.float32)]
         + [pltpu.VMEM(eigenbasis_columns.shape, jnp.float32) for _ in range(2)]
-        + [pltpu.SemaphoreType.DMA((2,))],
+        + [rate_scratch, pltpu.SemaphoreType.DMA((5,))],
     )(flags, last, seg_index.astype(jnp.int32).reshape(1), seg_tot, mine, prior_expectation,
-      update_weights, sampled_data, eigenbasis_columns, measuring_operator, params)
+      update_weights, sampled_data, eigenbasis_columns, measuring_operator, *rates)
     return (states, fitted)
 
 

time: 60.6 us -> 58.6 us (0.967)
  local copies, waits for them, and re-layouts: 2.63 us -> 0 us
  Pallas kernels: 16.7 us -> 17.5 us
    unnamed x8 -> x0, local copies, waits for them, and re-layouts: 2.59 us -> none
    pallas_call x1, Pallas kernels: 9.51 us -> 10.1 us  [on_device(): pl.pallas_call(final_kernel, out_shape=(out_block, out_block), in_specs=[...]
where the time goes in v6:
time: 58.6 us; the launch traced here: 58.2 us
  blocking collectives  40.1 us (68%)
  Pallas kernels  17.5 us (30%)
  between operations  0.65 us (1%)
    all_to_all x2, blocking collectives, gathered_over(): return lax.all_to_all(spread, axis, 0, 0, tiled=False)  40.1 us
    pallas_call x1, Pallas kernels, on_device(): pl.pallas_call(final_kernel, out_shape=(out_block, out_block), in_specs=[...  10.1 us
    pallas_call x1, Pallas kernels, on_device(): pl.pallas_call(summary_kernel, out_shape=jax.ShapeDtypeStruct((lax.axis_s...  5.28 us
    pallas_call x1, Pallas kernels, on_device(): pl.pallas_call(segment_kernel, out_shape=(jax.ShapeDtypeStruct((lax.axis_...  2.06 us

profile of v6, /device:TPU:1, one launch (start us, length us, event | category | flops | bytes accessed | tf_op | source)
XLA Modules:
  0.0 58.2 jit_solution(4714375837361071127)
XLA Ops:
  0.6 5.3 %shard_map.104 = f32[32,10,4,128]{3,2,1,0:T(4,128)} custom-call(s32[256]{0:T(256)} %flags_ref.3, s32[1]{0:T(128)} %bitcast.last_ref, f32[4,256,256]{2,1,0:T(8,128)} %w_ref.3, f32[4,256,256]{2,1,0:T(8,128)} %d_ref.3, f32[1,4,128]{2,1,0:T(4,128)} %fd_hbm.3, f32[1,4,128]{2,1,0:T(4,128)} %bd_hbm.3, f32[1,4,128]{2,1,0:T(4,128)} %th_hbm.3), custom_call_target="tpu_custom_call" | custom-call | tf_op jit(solution)/shard_map/pallas_call | solution.py:287
  5.9 21.6 %all_to_all.10.g_ref = f32[32,10,4,128]{3,2,1,0:T(4,128)} all-to-all(f32[32,10,4,128]{3,2,1,0:T(4,128)} %shard_map.104), channel_id=1, replica_groups=mesh['seg'=8,'blk'=32] {'blk'}, dimensions={0} | all-to-all | bytes 1310720 | tf_op jit(solution)/shard_map/all_to_all | solution.py:261
  27.5 2.1 %shard_map.105 = (f32[8,10,4,128]{3,2,1,0:T(4,128)}, f32[10,4,128]{2,1,0:T(4,128)}) custom-call(s32[1]{0:T(128)} %bitcast.2.me_ref, f32[32,10,4,128]{3,2,1,0:T(4,128)} %all_to_all.10.g_ref), custom_call_target="tpu_custom_call" | custom-call | tf_op jit(solution)/shard_map/pallas_call | solution.py:298
  29.6 18.5 %all_to_all.11.tot_ref = f32[8,10,4,128]{3,2,1,0:T(4,128)} all-to-all(f32[8,10,4,128]{3,2,1,0:T(4,128)} %get-tuple-element.4), channel_id=1, replica_groups=mesh['seg'=8,'blk'=32] {'seg'}, dimensions={0} | all-to-all | bytes 327680 | tf_op jit(solution)/shard_map/all_to_all | solution.py:261
  48.0 10.1 %shard_map.106 = (bf16[4,256,256]{2,1,0:T(8,128)(2,1)}, bf16[4,256,256]{2,1,0:T(8,128)(2,1)}) custom-call(s32[256]{0:T(256)} %flags_ref.3, s32[1]{0:T(128)} %bitcast.last_ref, s32[1]{0:T(128)} %bitcast.1.myseg_ref, f32[8,10,4,128]{3,2,1,0:T(4,128)} %all_to_all.11.tot_ref, f32[10,4,128]{2,1,0:T(4,128)} %get-tuple-element.5.mine_ref, f32[2,4,128]{2,1,0:T(4,128)} %prior_ref.1, ...), custom_call_target="tpu_custom_call" | custom-call | tf_op jit(solution)/shard_map/pallas_call | solution.py:311

commit v7 on v6

--- a/solution.py
+++ b/solution.py
@@ -72,15 +72,29 @@
     return one(xh, yh) + (one(xh, yl) + one(xl, yh))
 
 
-def fill_drive(w_ref, d_ref, u_ref):
+def start_input_copies(w_hbm, d_hbm, w_ref, d_ref, sems, first):
+    copies = []
     for a in range(w_ref.shape[0]):
+        pair = (pltpu.make_async_copy(w_hbm.at[a], w_ref.at[a], sems.at[first + 2 * a]),
+                pltpu.make_async_copy(d_hbm.at[a], d_ref.at[a], sems.at[first + 2 * a + 1]))
+        for c in pair:
+            c.start()
+        copies.append(pair)
+    return copies
+
+
+def fill_drive(w_ref, d_ref, u_ref, copies):
+    for a in range(w_ref.shape[0]):
+        for c in copies[a]:
+            c.wait()
         u_ref[:, a, :] = dot3(d_ref[a], w_ref[a], (((0,), (1,)), ((), ())))
 
 
-def summary_kernel(flags_ref, last_ref, w_ref, d_ref, fd_hbm, bd_hbm, th_hbm, out_ref, u_ref,
-                   rate_ref, sems):
+def summary_kernel(flags_ref, last_ref, w_hbm, d_hbm, fd_hbm, bd_hbm, th_hbm, out_ref, u_ref,
+                   rate_ref, w_ref, d_ref, sems):
+    inputs = start_input_copies(w_hbm, d_hbm, w_ref, d_ref, sems, 3)
     copies = start_rate_copies((fd_hbm, bd_hbm, th_hbm), rate_ref, sems, 0)
-    fill_drive(w_ref, d_ref, u_ref)
+    fill_drive(w_ref, d_ref, u_ref, inputs)
     for c in copies:
         c.wait()
     steps = u_ref.shape[0]
@@ -166,15 +180,16 @@
         mine_ref[idx] = v
 
 
-def final_kernel(flags_ref, last_ref, myseg_ref, tot_ref, mine_ref, prior_ref, w_ref, d_ref, e_hbm,
+def final_kernel(flags_ref, last_ref, myseg_ref, tot_ref, mine_ref, prior_ref, w_hbm, d_hbm, e_hbm,
                  o_hbm, fd_hbm, bd_hbm, th_hbm, states_ref, fitted_ref, u_ref, m_r, m_i, out_ref, e_ref,
-                 o_ref, rate_ref, sems):
+                 o_ref, rate_ref, w_ref, d_ref, sems):
+    inputs = start_input_copies(w_hbm, d_hbm, w_ref, d_ref, sems, 5)
     e_copy = pltpu.make_async_copy(e_hbm, e_ref, sems.at[0])
     o_copy = pltpu.make_async_copy(o_hbm, o_ref, sems.at[1])
     e_copy.start()
     o_copy.start()
     copies = start_rate_copies((fd_hbm, bd_hbm, th_hbm), rate_ref, sems, 2)
-    fill_drive(w_ref, d_ref, u_ref)
+    fill_drive(w_ref, d_ref, u_ref, inputs)
     steps = u_ref.shape[0]
     half = u_ref.shape[2] // 2
     segs = tot_ref.shape[0]
@@ -287,10 +302,11 @@
     summary = pl.pallas_call(
         summary_kernel,
         out_shape=jax.ShapeDtypeStruct((lax.axis_size("blk"), 10) + mode_shape, jnp.float32),
-        in_specs=[pl.BlockSpec(memory_space=SMEM)] * 2 + [pl.BlockSpec(memory_space=VMEM)] * 2
-        + [pl.BlockSpec(memory_space=pl.ANY)] * 3,
+        in_specs=[pl.BlockSpec(memory_space=SMEM)] * 2 + [pl.BlockSpec(memory_space=pl.ANY)] * 5,
         out_specs=pl.BlockSpec(memory_space=VMEM),
-        scratch_shapes=[pltpu.VMEM(u_shape, jnp.float32), rate_scratch, pltpu.SemaphoreType.DMA((3,))],
+        scratch_shapes=[pltpu.VMEM(u_shape, jnp.float32), rate_scratch]
+        + [pltpu.VMEM(update_weights.shape, jnp.float32), pltpu.VMEM(sampled_data.shape, jnp.float32)]
+        + [pltpu.SemaphoreType.DMA((11,))],
     )(flags, last, update_weights, sampled_data, *rates)
 
     gathered = gathered_over(summary, "blk")
@@ -311,14 +327,16 @@
     states, fitted = pl.pallas_call(
         final_kernel,
         out_shape=(out_block, out_block),
-        in_specs=[pl.BlockSpec(memory_space=SMEM)] * 3 + [pl.BlockSpec(memory_space=VMEM)] * 5
-        + [pl.BlockSpec(memory_space=pl.ANY)] * 5,
+        in_specs=[pl.BlockSpec(memory_space=SMEM)] * 3 + [pl.BlockSpec(memory_space=VMEM)] * 3
+        + [pl.BlockSpec(memory_space=pl.ANY)] * 7,
         out_specs=(pl.BlockSpec(memory_space=VMEM), pl.BlockSpec(memory_space=VMEM)),
         scratch_shapes=[pltpu.VMEM(u_shape, jnp.float32)]
         + [pltpu.VMEM((steps,) + mode_shape, jnp.float32) for _ in range(2)]
         + [pltpu.VMEM(u_shape, jnp.float32)]
         + [pltpu.VMEM(eigenbasis_columns.shape, jnp.float32) for _ in range(2)]
-        + [rate_scratch, pltpu.SemaphoreType.DMA((5,))],
+        + [rate_scratch]
+        + [pltpu.VMEM(update_weights.shape, jnp.float32), pltpu.VMEM(sampled_data.shape, jnp.float32)]
+        + [pltpu.SemaphoreType.DMA((13,))],
     )(flags, last, seg_index.astype(jnp.int32).reshape(1), seg_tot, mine, prior_expectation,
       update_weights, sampled_data, eigenbasis_columns, measuring_operator, *rates)
     return (states, fitted)

time: 58.6 us -> 60.4 us (1.031)
  Pallas kernels: 17.5 us -> 19.3 us
    pallas_call x1, Pallas kernels: 5.28 us -> 6.39 us  [on_device(): pl.pallas_call(summary_kernel, out_shape=jax.ShapeDtypeStruct((lax.axis_s...]
    pallas_call x1, Pallas kernels: 10.1 us -> 10.8 us  [on_device(): pl.pallas_call(final_kernel, out_shape=(out_block, out_block), in_specs=[...]
where the time goes in v7:
time: 60.4 us; the launch traced here: 60 us
  blocking collectives  40.1 us (66%)
  Pallas kernels  19.3 us (32%)
  between operations  0.65 us (1%)
    all_to_all x2, blocking collectives, gathered_over(): return lax.all_to_all(spread, axis, 0, 0, tiled=False)  40.1 us
    pallas_call x1, Pallas kernels, on_device(): pl.pallas_call(final_kernel, out_shape=(out_block, out_block), in_specs=[...  10.8 us
    pallas_call x1, Pallas kernels, on_device(): pl.pallas_call(summary_kernel, out_shape=jax.ShapeDtypeStruct((lax.axis_s...  6.39 us
    pallas_call x1, Pallas kernels, on_device(): pl.pallas_call(segment_kernel, out_shape=(jax.ShapeDtypeStruct((lax.axis_...  2.06 us

profile of v7, /device:TPU:1, one launch (start us, length us, event | category | flops | bytes accessed | tf_op | source)
XLA Modules:
  0.0 60.0 jit_solution(11901626835193562264)
XLA Ops:
  0.6 6.4 %shard_map.104 = f32[32,10,4,128]{3,2,1,0:T(4,128)} custom-call(s32[256]{0:T(256)} %flags_ref.3, s32[1]{0:T(128)} %bitcast.last_ref, f32[4,256,256]{2,1,0:T(8,128)} %w_hbm.3, f32[4,256,256]{2,1,0:T(8,128)} %d_hbm.3, f32[1,4,128]{2,1,0:T(4,128)} %fd_hbm.3, f32[1,4,128]{2,1,0:T(4,128)} %bd_hbm.3, f32[1,4,128]{2,1,0:T(4,128)} %th_hbm.3), custom_call_target="tpu_custom_call" | custom-call | tf_op jit(solution)/shard_map/pallas_call | solution.py:302
  7.0 21.6 %all_to_all.10.g_ref = f32[32,10,4,128]{3,2,1,0:T(4,128)} all-to-all(f32[32,10,4,128]{3,2,1,0:T(4,128)} %shard_map.104), channel_id=1, replica_groups=mesh['seg'=8,'blk'=32] {'blk'}, dimensions={0} | all-to-all | bytes 1310720 | tf_op jit(solution)/shard_map/all_to_all | solution.py:276
  28.6 2.1 %shard_map.105 = (f32[8,10,4,128]{3,2,1,0:T(4,128)}, f32[10,4,128]{2,1,0:T(4,128)}) custom-call(s32[1]{0:T(128)} %bitcast.2.me_ref, f32[32,10,4,128]{3,2,1,0:T(4,128)} %all_to_all.10.g_ref), custom_call_target="tpu_custom_call" | custom-call | tf_op jit(solution)/shard_map/pallas_call | solution.py:314
  30.7 18.5 %all_to_all.11.tot_ref = f32[8,10,4,128]{3,2,1,0:T(4,128)} all-to-all(f32[8,10,4,128]{3,2,1,0:T(4,128)} %get-tuple-element.4), channel_id=1, replica_groups=mesh['seg'=8,'blk'=32] {'seg'}, dimensions={0} | all-to-all | bytes 327680 | tf_op jit(solution)/shard_map/all_to_all | solution.py:276
  49.2 10.8 %shard_map.106 = (bf16[4,256,256]{2,1,0:T(8,128)(2,1)}, bf16[4,256,256]{2,1,0:T(8,128)(2,1)}) custom-call(s32[256]{0:T(256)} %flags_ref.3, s32[1]{0:T(128)} %bitcast.last_ref, s32[1]{0:T(128)} %bitcast.1.myseg_ref, f32[8,10,4,128]{3,2,1,0:T(4,128)} %all_to_all.11.tot_ref, f32[10,4,128]{2,1,0:T(4,128)} %get-tuple-element.5.mine_ref, f32[2,4,128]{2,1,0:T(4,128)} %prior_ref.1, ...), custom_call_target="tpu_custom_call" | custom-call | tf_op jit(solution)/shard_map/pallas_call | solution.py:327

commit v8 on v6

--- a/solution.py
+++ b/solution.py
@@ -115,7 +115,7 @@
         return (mr, mi, ar, ai, pr, pi, qr, qi, hr, hi)
 
     carry = (zero, zero, one, zero, zero, zero, zero, zero, one, zero)
-    carry = lax.fori_loop(0, steps - 1, lambda t, c: step(t, c, False), carry, unroll=8)
+    carry = lax.fori_loop(0, steps - 1, lambda t, c: step(t, c, False), carry, unroll=32)
     carry = step(steps - 1, carry, True)
     mr, mi, ar, ai, pr, pi, qr, qi, hr, hi = carry
     for idx, v in enumerate((ar, ai, mr, mi, hr, hi, pr, pi, qr, qi)):
@@ -224,7 +224,7 @@
         m_i[t] = mi
         return (mr, mi)
 
-    lax.fori_loop(0, steps, fwd, (cr, ci), unroll=8)
+    lax.fori_loop(0, steps, fwd, (cr, ci), unroll=32)
 
     def bwd_step(t, carry, final):
         sr, si = carry
@@ -244,7 +244,7 @@
         return (sr, si)
 
     carry = bwd_step(steps - 1, (er, ei), True)
-    lax.fori_loop(0, steps - 1, lambda j, c: bwd_step(steps - 2 - j, c, False), carry, unroll=8)
+    lax.fori_loop(0, steps - 1, lambda j, c: bwd_step(steps - 2 - j, c, False), carry, unroll=32)
 
     e_copy.wait()
     o_copy.wait()

time: 58.6 us -> 58.6 us (level)
  no operation moved by 1% of the time
where the time goes in v8:
time: 58.6 us; the launch traced here: 58.2 us
  blocking collectives  40.1 us (68%)
  Pallas kernels  17.5 us (30%)
  between operations  0.65 us (1%)
    all_to_all x2, blocking collectives, gathered_over(): return lax.all_to_all(spread, axis, 0, 0, tiled=False)  40.1 us
    pallas_call x1, Pallas kernels, on_device(): pl.pallas_call(final_kernel, out_shape=(out_block, out_block), in_specs=[...  10.1 us
    pallas_call x1, Pallas kernels, on_device(): pl.pallas_call(summary_kernel, out_shape=jax.ShapeDtypeStruct((lax.axis_s...  5.39 us
    pallas_call x1, Pallas kernels, on_device(): pl.pallas_call(segment_kernel, out_shape=(jax.ShapeDtypeStruct((lax.axis_...  2.06 us

profile of v8, /device:TPU:1, one launch (start us, length us, event | category | flops | bytes accessed | tf_op | source)
XLA Modules:
  0.0 58.2 jit_solution(13214072554759658927)
XLA Ops:
  0.6 5.4 %shard_map.104 = f32[32,10,4,128]{3,2,1,0:T(4,128)} custom-call(s32[256]{0:T(256)} %flags_ref.3, s32[1]{0:T(128)} %bitcast.last_ref, f32[4,256,256]{2,1,0:T(8,128)} %w_ref.3, f32[4,256,256]{2,1,0:T(8,128)} %d_ref.3, f32[1,4,128]{2,1,0:T(4,128)} %fd_hbm.3, f32[1,4,128]{2,1,0:T(4,128)} %bd_hbm.3, f32[1,4,128]{2,1,0:T(4,128)} %th_hbm.3), custom_call_target="tpu_custom_call" | custom-call | tf_op jit(solution)/shard_map/pallas_call | solution.py:287
  6.0 21.6 %all_to_all.10.g_ref = f32[32,10,4,128]{3,2,1,0:T(4,128)} all-to-all(f32[32,10,4,128]{3,2,1,0:T(4,128)} %shard_map.104), channel_id=1, replica_groups=mesh['seg'=8,'blk'=32] {'blk'}, dimensions={0} | all-to-all | bytes 1310720 | tf_op jit(solution)/shard_map/all_to_all | solution.py:261
  27.6 2.1 %shard_map.105 = (f32[8,10,4,128]{3,2,1,0:T(4,128)}, f32[10,4,128]{2,1,0:T(4,128)}) custom-call(s32[1]{0:T(128)} %bitcast.2.me_ref, f32[32,10,4,128]{3,2,1,0:T(4,128)} %all_to_all.10.g_ref), custom_call_target="tpu_custom_call" | custom-call | tf_op jit(solution)/shard_map/pallas_call | solution.py:298
  29.7 18.5 %all_to_all.11.tot_ref = f32[8,10,4,128]{3,2,1,0:T(4,128)} all-to-all(f32[8,10,4,128]{3,2,1,0:T(4,128)} %get-tuple-element.4), channel_id=1, replica_groups=mesh['seg'=8,'blk'=32] {'seg'}, dimensions={0} | all-to-all | bytes 327680 | tf_op jit(solution)/shard_map/all_to_all | solution.py:261
  48.2 10.1 %shard_map.106 = (bf16[4,256,256]{2,1,0:T(8,128)(2,1)}, bf16[4,256,256]{2,1,0:T(8,128)(2,1)}) custom-call(s32[256]{0:T(256)} %flags_ref.3, s32[1]{0:T(128)} %bitcast.last_ref, s32[1]{0:T(128)} %bitcast.1.myseg_ref, f32[8,10,4,128]{3,2,1,0:T(4,128)} %all_to_all.11.tot_ref, f32[10,4,128]{2,1,0:T(4,128)} %get-tuple-element.5.mine_ref, f32[2,4,128]{2,1,0:T(4,128)} %prior_ref.1, ...), custom_call_target="tpu_custom_call" | custom-call | tf_op jit(solution)/shard_map/pallas_call | solution.py:311

commit v9 on v6

--- a/solution.py
+++ b/solution.py
@@ -77,8 +77,8 @@
         u_ref[:, a, :] = dot3(d_ref[a], w_ref[a], (((0,), (1,)), ((), ())))
 
 
-def summary_kernel(flags_ref, last_ref, w_ref, d_ref, fd_hbm, bd_hbm, th_hbm, out_ref, u_ref,
-                   rate_ref, sems):
+def summary_kernel(flags_ref, last_ref, w_ref, d_ref, fd_hbm, bd_hbm, th_hbm, out_ref, b_ref, a_ref,
+                   u_ref, rate_ref, sems):
     copies = start_rate_copies((fd_hbm, bd_hbm, th_hbm), rate_ref, sems, 0)
     fill_drive(w_ref, d_ref, u_ref)
     for c in copies:
@@ -98,6 +98,10 @@
         u = u_ref[t]
         mr, mi = lr * mr - li * mi + scale * u[:, :half], lr * mi + li * mr + scale * u[:, half:]
         ar, ai = cmul(lr, li, ar, ai)
+        b_ref[t, :, :half] = mr
+        b_ref[t, :, half:] = mi
+        a_ref[t, :, :half] = ar
+        a_ref[t, :, half:] = ai
         w = jnp.where(flag == 1, w_spike, w_plain)
         br, bi = f * bk_r, f * bk_i
         if final:
@@ -166,17 +170,18 @@
         mine_ref[idx] = v
 
 
-def final_kernel(flags_ref, last_ref, myseg_ref, tot_ref, mine_ref, prior_ref, w_ref, d_ref, e_hbm,
-                 o_hbm, fd_hbm, bd_hbm, th_hbm, states_ref, fitted_ref, u_ref, m_r, m_i, out_ref, e_ref,
+def final_kernel(flags_ref, last_ref, myseg_ref, tot_ref, mine_ref, prior_ref, b_ref, a_ref, d_hbm,
+                 e_hbm, o_hbm, fd_hbm, bd_hbm, th_hbm, states_ref, fitted_ref, out_ref, d_ref, e_ref,
                  o_ref, rate_ref, sems):
     e_copy = pltpu.make_async_copy(e_hbm, e_ref, sems.at[0])
     o_copy = pltpu.make_async_copy(o_hbm, o_ref, sems.at[1])
+    d_copy = pltpu.make_async_copy(d_hbm, d_ref, sems.at[5])
     e_copy.start()
     o_copy.start()
+    d_copy.start()
     copies = start_rate_copies((fd_hbm, bd_hbm, th_hbm), rate_ref, sems, 2)
-    fill_drive(w_ref, d_ref, u_ref)
-    steps = u_ref.shape[0]
-    half = u_ref.shape[2] // 2
+    steps = b_ref.shape[0]
+    half = b_ref.shape[2] // 2
     segs = tot_ref.shape[0]
     myseg = myseg_ref[0]
     zero = jnp.zeros(prior_ref.shape[1:], jnp.float32)
@@ -214,18 +219,6 @@
     lam_r, lam_i, bk_r, bk_i, w_plain, w_spike, scale = mode_params(
         rate_ref[0, 0], rate_ref[1, 0], rate_ref[2, 0])
 
-    def fwd(t, carry):
-        mr, mi = carry
-        f = factor_of(flags_ref[t])
-        lr, li = f * lam_r, f * lam_i
-        u = u_ref[t]
-        mr, mi = lr * mr - li * mi + scale * u[:, :half], lr * mi + li * mr + scale * u[:, half:]
-        m_r[t] = mr
-        m_i[t] = mi
-        return (mr, mi)
-
-    lax.fori_loop(0, steps, fwd, (cr, ci), unroll=8)
-
     def bwd_step(t, carry, final):
         sr, si = carry
         flag = flags_ref[t]
@@ -237,8 +230,11 @@
             w = jnp.where(last, one, w)
             br = jnp.where(last, zero, br)
             bi = jnp.where(last, zero, bi)
+        b = b_ref[t]
+        a = a_ref[t]
+        xr, xi = cmul(a[:, :half], a[:, half:], cr, ci)
         nr, ni = cmul(br, bi, sr, si)
-        sr, si = nr + w * m_r[t], ni + w * m_i[t]
+        sr, si = nr + w * (b[:, :half] + xr), ni + w * (b[:, half:] + xi)
         out_ref[t, :, :half] = sr
         out_ref[t, :, half:] = si
         return (sr, si)
@@ -248,6 +244,7 @@
 
     e_copy.wait()
     o_copy.wait()
+    d_copy.wait()
     contract = (((1,), (1,)), ((), ()))
     for a in range(e_ref.shape[0]):
         stacked = out_ref[:, a, :]
@@ -284,12 +281,13 @@
     rate_scratch = pltpu.VMEM((3,) + eigen_damping.shape, jnp.float32)
 
     mode_shape = eigen_damping.shape[1:]
-    summary = pl.pallas_call(
+    runs = jax.ShapeDtypeStruct(u_shape, jnp.float32)
+    summary, forward_zero, growth = pl.pallas_call(
         summary_kernel,
-        out_shape=jax.ShapeDtypeStruct((lax.axis_size("blk"), 10) + mode_shape, jnp.float32),
+        out_shape=(jax.ShapeDtypeStruct((lax.axis_size("blk"), 10) + mode_shape, jnp.float32), runs, runs),
         in_specs=[pl.BlockSpec(memory_space=SMEM)] * 2 + [pl.BlockSpec(memory_space=VMEM)] * 2
         + [pl.BlockSpec(memory_space=pl.ANY)] * 3,
-        out_specs=pl.BlockSpec(memory_space=VMEM),
+        out_specs=(pl.BlockSpec(memory_space=VMEM),) * 3,
         scratch_shapes=[pltpu.VMEM(u_shape, jnp.float32), rate_scratch, pltpu.SemaphoreType.DMA((3,))],
     )(flags, last, update_weights, sampled_data, *rates)
 
@@ -312,15 +310,14 @@
         final_kernel,
         out_shape=(out_block, out_block),
         in_specs=[pl.BlockSpec(memory_space=SMEM)] * 3 + [pl.BlockSpec(memory_space=VMEM)] * 5
-        + [pl.BlockSpec(memory_space=pl.ANY)] * 5,
+        + [pl.BlockSpec(memory_space=pl.ANY)] * 6,
         out_specs=(pl.BlockSpec(memory_space=VMEM), pl.BlockSpec(memory_space=VMEM)),
         scratch_shapes=[pltpu.VMEM(u_shape, jnp.float32)]
-        + [pltpu.VMEM((steps,) + mode_shape, jnp.float32) for _ in range(2)]
-        + [pltpu.VMEM(u_shape, jnp.float32)]
+        + [pltpu.VMEM(sampled_data.shape, jnp.float32)]
         + [pltpu.VMEM(eigenbasis_columns.shape, jnp.float32) for _ in range(2)]
-        + [rate_scratch, pltpu.SemaphoreType.DMA((5,))],
+        + [rate_scratch, pltpu.SemaphoreType.DMA((6,))],
     )(flags, last, seg_index.astype(jnp.int32).reshape(1), seg_tot, mine, prior_expectation,
-      update_weights, sampled_data, eigenbasis_columns, measuring_operator, *rates)
+      forward_zero, growth, sampled_data, eigenbasis_columns, measuring_operator, *rates)
     return (states, fitted)
 
 

time: 58.6 us -> 58.7 us (level)
    pallas_call x1, Pallas kernels: 5.28 us -> 6.02 us  [on_device(): pl.pallas_call(summary_kernel, out_shape=(jax.ShapeDtypeStruct((lax.axis_...]
    pallas_call x1, Pallas kernels: 10.1 us -> 9.49 us  [on_device(): pl.pallas_call(final_kernel, out_shape=(out_block, out_block), in_specs=[...]
where the time goes in v9:
time: 58.7 us; the launch traced here: 58.3 us
  blocking collectives  40.1 us (68%)
  Pallas kernels  17.6 us (30%)
  between operations  0.65 us (1%)
    all_to_all x2, blocking collectives, gathered_over(): return lax.all_to_all(spread, axis, 0, 0, tiled=False)  40.1 us
    pallas_call x1, Pallas kernels, on_device(): pl.pallas_call(final_kernel, out_shape=(out_block, out_block), in_specs=[...  9.49 us
    pallas_call x1, Pallas kernels, on_device(): pl.pallas_call(summary_kernel, out_shape=(jax.ShapeDtypeStruct((lax.axis_...  6.02 us
    pallas_call x1, Pallas kernels, on_device(): pl.pallas_call(segment_kernel, out_shape=(jax.ShapeDtypeStruct((lax.axis_...  2.06 us

profile of v9, /device:TPU:1, one launch (start us, length us, event | category | flops | bytes accessed | tf_op | source)
XLA Modules:
  0.0 58.3 jit_solution(2912800066504855202)
XLA Ops:
  0.6 6.0 %shard_map.104 = (f32[32,10,4,128]{3,2,1,0:T(4,128)}, f32[256,4,256]{2,1,0:T(4,128)}, f32[256,4,256]{2,1,0:T(4,128)}) custom-call(s32[256]{0:T(256)} %flags_ref.3, s32[1]{0:T(128)} %bitcast.last_ref, f32[4,256,256]{2,1,0:T(8,128)} %w_ref.1, f32[4,256,256]{2,1,0:T(8,128)} %d_hbm.1, f32[1,4,128]{2,1,0:T(4,128)} %fd_hbm.3, f32[1,4,128]{2,1,0:T(4,128)} %bd_hbm.3, ...), custom_call_target="tpu_custom_call" | custom-call | tf_op jit(solution)/shard_map/pallas_call | solution.py:285
  6.7 21.6 %all_to_all.10.g_ref = f32[32,10,4,128]{3,2,1,0:T(4,128)} all-to-all(f32[32,10,4,128]{3,2,1,0:T(4,128)} %get-tuple-element.7), channel_id=1, replica_groups=mesh['seg'=8,'blk'=32] {'blk'}, dimensions={0} | all-to-all | bytes 1310720 | tf_op jit(solution)/shard_map/all_to_all | solution.py:258
  28.3 2.1 %shard_map.105 = (f32[8,10,4,128]{3,2,1,0:T(4,128)}, f32[10,4,128]{2,1,0:T(4,128)}) custom-call(s32[1]{0:T(128)} %bitcast.2.me_ref, f32[32,10,4,128]{3,2,1,0:T(4,128)} %all_to_all.10.g_ref), custom_call_target="tpu_custom_call" | custom-call | tf_op jit(solution)/shard_map/pallas_call | solution.py:296
  30.3 18.5 %all_to_all.11.tot_ref = f32[8,10,4,128]{3,2,1,0:T(4,128)} all-to-all(f32[8,10,4,128]{3,2,1,0:T(4,128)} %get-tuple-element.8), channel_id=1, replica_groups=mesh['seg'=8,'blk'=32] {'seg'}, dimensions={0} | all-to-all | bytes 327680 | tf_op jit(solution)/shard_map/all_to_all | solution.py:258
  48.8 9.5 %shard_map.106 = (bf16[4,256,256]{2,1,0:T(8,128)(2,1)}, bf16[4,256,256]{2,1,0:T(8,128)(2,1)}) custom-call(s32[256]{0:T(256)} %flags_ref.3, s32[1]{0:T(128)} %bitcast.last_ref, s32[1]{0:T(128)} %bitcast.1.myseg_ref, f32[8,10,4,128]{3,2,1,0:T(4,128)} %all_to_all.11.tot_ref, f32[10,4,128]{2,1,0:T(4,128)} %get-tuple-element.9.mine_ref, f32[2,4,128]{2,1,0:T(4,128)} %prior_ref.1, ...), custom_call_target="tpu_custom_call" | custom-call | tf_op jit(solution)/shard_map/pallas_call | solution.py:309

commit v10 on v6

--- a/solution.py
+++ b/solution.py
@@ -166,15 +166,18 @@
         mine_ref[idx] = v
 
 
-def final_kernel(flags_ref, last_ref, myseg_ref, tot_ref, mine_ref, prior_ref, w_ref, d_ref, e_hbm,
-                 o_hbm, fd_hbm, bd_hbm, th_hbm, states_ref, fitted_ref, u_ref, m_r, m_i, out_ref, e_ref,
+def drive_kernel(w_ref, d_ref, u_ref):
+    fill_drive(w_ref, d_ref, u_ref)
+
+
+def final_kernel(flags_ref, last_ref, myseg_ref, tot_ref, mine_ref, prior_ref, u_ref, d_ref, e_hbm,
+                 o_hbm, fd_hbm, bd_hbm, th_hbm, states_ref, fitted_ref, m_r, m_i, out_ref, e_ref,
                  o_ref, rate_ref, sems):
     e_copy = pltpu.make_async_copy(e_hbm, e_ref, sems.at[0])
     o_copy = pltpu.make_async_copy(o_hbm, o_ref, sems.at[1])
     e_copy.start()
     o_copy.start()
     copies = start_rate_copies((fd_hbm, bd_hbm, th_hbm), rate_ref, sems, 2)
-    fill_drive(w_ref, d_ref, u_ref)
     steps = u_ref.shape[0]
     half = u_ref.shape[2] // 2
     segs = tot_ref.shape[0]
@@ -306,6 +309,15 @@
         scratch_shapes=[pltpu.VMEM((count,) + mode_shape, jnp.float32) for _ in range(4)],
     )(blk_index.astype(jnp.int32).reshape(1), gathered)
 
+    drive = pl.pallas_call(
+        drive_kernel,
+        out_shape=jax.ShapeDtypeStruct(u_shape, jnp.float32),
+        in_specs=[pl.BlockSpec(memory_space=VMEM)] * 2,
+        out_specs=pl.BlockSpec(memory_space=VMEM),
+        cost_estimate=pl.CostEstimate(flops=3 * 2 * int(math.prod(sampled_data.shape)) * sampled_data.shape[1],
+                                      bytes_accessed=4 * 4 * int(math.prod(sampled_data.shape)),
+                                      transcendentals=0),
+    )(update_weights, sampled_data)
     seg_tot = gathered_over(tot, "seg")
     out_block = jax.ShapeDtypeStruct(sampled_data.shape, jnp.bfloat16)
     states, fitted = pl.pallas_call(
@@ -314,13 +326,12 @@
         in_specs=[pl.BlockSpec(memory_space=SMEM)] * 3 + [pl.BlockSpec(memory_space=VMEM)] * 5
         + [pl.BlockSpec(memory_space=pl.ANY)] * 5,
         out_specs=(pl.BlockSpec(memory_space=VMEM), pl.BlockSpec(memory_space=VMEM)),
-        scratch_shapes=[pltpu.VMEM(u_shape, jnp.float32)]
-        + [pltpu.VMEM((steps,) + mode_shape, jnp.float32) for _ in range(2)]
+        scratch_shapes=[pltpu.VMEM((steps,) + mode_shape, jnp.float32) for _ in range(2)]
         + [pltpu.VMEM(u_shape, jnp.float32)]
         + [pltpu.VMEM(eigenbasis_columns.shape, jnp.float32) for _ in range(2)]
         + [rate_scratch, pltpu.SemaphoreType.DMA((5,))],
     )(flags, last, seg_index.astype(jnp.int32).reshape(1), seg_tot, mine, prior_expectation,
-      update_weights, sampled_data, eigenbasis_columns, measuring_operator, *rates)
+      drive, sampled_data, eigenbasis_columns, measuring_operator, *rates)
     return (states, fitted)
 
 

time: 58.6 us -> 59.2 us (1.010)
  blocking collectives: 40.1 us -> 21.6 us
  starting transfers between devices: 0 us -> 8.19 us
  waiting for transfers between devices: 0 us -> 6.89 us
  Pallas kernels: 17.5 us -> 20.7 us
  local copies, waits for them, and re-layouts: 0 us -> 0.66 us
    all_to_all x2 -> x1, blocking collectives: 40.1 us -> 21.6 us  [gathered_over(): return lax.all_to_all(spread, axis, 0, 0, tiled=False)]
    all_to_all x0 -> x1, starting transfers between devices: none -> 8.19 us  [gathered_over(): return lax.all_to_all(spread, axis, 0, 0, tiled=False)]
    all_to_all x0 -> x1, waiting for transfers between devices: none -> 6.89 us  [gathered_over(): return lax.all_to_all(spread, axis, 0, 0, tiled=False)]
    pallas_call x0 -> x1, Pallas kernels: none -> 3.28 us  [on_device(): pl.pallas_call(drive_kernel, out_shape=jax.ShapeDtypeStruct(u_shape, jnp....]
    unnamed x0 -> x2, local copies, waits for them, and re-layouts: none -> 0.66 us
  transfers between devices with their start and end apart: 0 -> 1, of which waited for: 0 -> 1; matrix products, arithmetic and copies ran while one was open for 0% -> 0% of each run, Pallas kernels for 0% -> 6%
where the time goes in v10:
time: 59.2 us; the launch traced here: 58.7 us
  blocking collectives  21.6 us (36%)
  Pallas kernels  20.7 us (35%)
  starting transfers between devices  8.19 us (14%)
  waiting for transfers between devices  6.89 us (12%)
  local copies, waits for them, and re-layouts  0.66 us (1%)
  between operations  0.65 us (1%)
    all_to_all x1, blocking collectives, gathered_over(): return lax.all_to_all(spread, axis, 0, 0, tiled=False)  21.6 us
    pallas_call x1, Pallas kernels, on_device(): pl.pallas_call(final_kernel, out_shape=(out_block, out_block), in_specs=[...  10.1 us
    all_to_all x1, starting transfers between devices, gathered_over(): return lax.all_to_all(spread, axis, 0, 0, tiled=False)  8.19 us
    all_to_all x1, waiting for transfers between devices, gathered_over(): return lax.all_to_all(spread, axis, 0, 0, tiled=False)  6.89 us
    pallas_call x1, Pallas kernels, on_device(): pl.pallas_call(summary_kernel, out_shape=jax.ShapeDtypeStruct((lax.axis_s...  5.26 us
    pallas_call x1, Pallas kernels, on_device(): pl.pallas_call(drive_kernel, out_shape=jax.ShapeDtypeStruct(u_shape, jnp....  3.28 us
    pallas_call x1, Pallas kernels, on_device(): pl.pallas_call(segment_kernel, out_shape=(jax.ShapeDtypeStruct((lax.axis_...  2.06 us
  transfers between devices with their start and end apart: 1, of which 1 were waited for; matrix products, arithmetic and copies ran while one was open for 0% of the time, Pallas kernels for 6%

profile of v10, /device:TPU:1, one launch (start us, length us, event | category | flops | bytes accessed | tf_op | source)
XLA Modules:
  0.0 58.7 jit_solution(8817379903976945372)
XLA Ops:
  0.6 5.3 %shard_map.104 = f32[32,10,4,128]{3,2,1,0:T(4,128)} custom-call(s32[256]{0:T(256)} %flags_ref.3, s32[1]{0:T(128)} %bitcast.last_ref, f32[4,256,256]{2,1,0:T(8,128)} %w_ref.3, f32[4,256,256]{2,1,0:T(8,128)} %d_ref.5, f32[1,4,128]{2,1,0:T(4,128)} %fd_hbm.3, f32[1,4,128]{2,1,0:T(4,128)} %bd_hbm.3, f32[1,4,128]{2,1,0:T(4,128)} %th_hbm.3), custom_call_target="tpu_custom_call" | custom-call | tf_op jit(solution)/shard_map/pallas_call | solution.py:290
  5.9 21.6 %all_to_all.10.g_ref = f32[32,10,4,128]{3,2,1,0:T(4,128)} all-to-all(f32[32,10,4,128]{3,2,1,0:T(4,128)} %shard_map.104), channel_id=1, replica_groups=mesh['seg'=8,'blk'=32] {'blk'}, dimensions={0} | all-to-all | bytes 1310720 | tf_op jit(solution)/shard_map/all_to_all | solution.py:264
  27.5 2.1 %shard_map.105 = (f32[8,10,4,128]{3,2,1,0:T(4,128)}, f32[10,4,128]{2,1,0:T(4,128)}) custom-call(s32[1]{0:T(128)} %bitcast.2.me_ref, f32[32,10,4,128]{3,2,1,0:T(4,128)} %all_to_all.10.g_ref), custom_call_target="tpu_custom_call" | custom-call | tf_op jit(solution)/shard_map/pallas_call | solution.py:301
  29.6 8.2 %all-to-all-start.1 = ((f32[8,10,4,128]{3,2,1,0:T(4,128)}), f32[8,10,4,128]{3,2,1,0:T(4,128)S(1)}, u32[]{:S(2)}, u32[]{:S(2)}) async-start(f32[8,10,4,128]{3,2,1,0:T(4,128)} %get-tuple-element.4), calls=%async_computation.1 | async-start | bytes 327680 | tf_op jit(solution)/shard_map/all_to_all | solution.py:264
  37.8 3.3 %shard_map.106.u_ref = f32[256,4,256]{2,1,0:T(4,128)} custom-call(f32[4,256,256]{2,1,0:T(8,128)} %w_ref.3, f32[4,256,256]{2,1,0:T(8,128)} %d_ref.5), custom_call_target="tpu_custom_call" | custom-call | flops 402653184 | bytes 4194304 | tf_op jit(solution)/shard_map/pallas_call | solution.py:312
  41.0 6.9 %all-to-all-done.1.tot_ref = f32[8,10,4,128]{3,2,1,0:T(4,128)S(1)} async-done(((f32[8,10,4,128]{3,2,1,0:T(4,128)}), f32[8,10,4,128]{3,2,1,0:T(4,128)S(1)}, u32[]{:S(2)}, u32[]{:S(2)}) %all-to-all-start.1) | async-done | bytes 163872 | tf_op jit(solution)/shard_map/all_to_all | solution.py:264
  47.9 0.0 copy-start
  47.9 0.7 %copy-done = f32[8,10,4,128]{3,2,1,0:T(4,128)} copy-done((f32[8,10,4,128]{3,2,1,0:T(4,128)}, f32[8,10,4,128]{3,2,1,0:T(4,128)S(1)}, u32[]{:S(2)}) %copy-start) | copy-done | bytes 163864
  48.6 10.1 %shard_map.107 = (bf16[4,256,256]{2,1,0:T(8,128)(2,1)}, bf16[4,256,256]{2,1,0:T(8,128)(2,1)}) custom-call(s32[256]{0:T(256)} %flags_ref.3, s32[1]{0:T(128)} %bitcast.last_ref, s32[1]{0:T(128)} %bitcast.1.myseg_ref, f32[8,10,4,128]{3,2,1,0:T(4,128)} %copy-done, f32[10,4,128]{2,1,0:T(4,128)} %get-tuple-element.5.mine_ref, f32[2,4,128]{2,1,0:T(4,128)} %prior_ref.1, ...), custom_call_target="tpu_custom_call" | custom-call | tf_op jit(solution)/shard_map/pallas_call | solution.py:323
Async XLA Ops:
  29.6 18.4 %all-to-all-start.1 = ((f32[8,10,4,128]{3,2,1,0:T(4,128)}), f32[8,10,4,128]{3,2,1,0:T(4,128)S(1)}, u32[]{:S(2)}, u32[]{:S(2)}) async-start(f32[8,10,4,128]{3,2,1,0:T(4,128)} %get-tuple-element.4), calls=%async_computation.1 | async-start | bytes 327680 | tf_op jit(solution)/shard_map/all_to_all | solution.py:264
  47.9 0.7 %copy-start = (f32[8,10,4,128]{3,2,1,0:T(4,128)}, f32[8,10,4,128]{3,2,1,0:T(4,128)S(1)}, u32[]{:S(2)}) copy-start(f32[8,10,4,128]{3,2,1,0:T(4,128)S(1)} %all-to-all-done.1.tot_ref) | copy-start | bytes 491524

commit v11 on v6

--- a/solution.py
+++ b/solution.py
@@ -123,30 +123,26 @@
             out_ref[k, idx] = v
 
 
-def segment_kernel(me_ref, g_ref, tot_ref, mine_ref, al_r, al_i, be_r, be_i):
+def segment_kernel(me_ref, g_ref, tot_ref, mine_ref, al_r, al_i, be_r, be_i, back_ref):
     count = g_ref.shape[0]
     me = me_ref[0]
     zero = jnp.zeros(g_ref.shape[2:], jnp.float32)
     one = jnp.ones_like(zero)
 
     ar, ai, br, bi = one, zero, zero, zero
-    rec = [one, zero, zero, zero]
     for k in range(count):
-        sel = me == k
-        rec = [jnp.where(sel, v, r) for v, r in zip((ar, ai, br, bi), rec)]
         al_r[k], al_i[k], be_r[k], be_i[k] = ar, ai, br, bi
         Ar, Ai, Br, Bi = g_ref[k, 0], g_ref[k, 1], g_ref[k, 2], g_ref[k, 3]
         ar, ai = cmul(Ar, Ai, ar, ai)
         nr, ni = cmul(Ar, Ai, br, bi)
         br, bi = nr + Br, ni + Bi
     fwd_tot = (ar, ai, br, bi)
-    fwd_me = rec
+    fwd_me = [al_r[me], al_i[me], be_r[me], be_i[me]]
 
     gr, gi, pr, pi, kr, ki = one, zero, zero, zero, zero, zero
-    rec = [one, zero, zero, zero, zero, zero]
     for k in reversed(range(count)):
-        sel = me == k
-        rec = [jnp.where(sel, v, r) for v, r in zip((gr, gi, pr, pi, kr, ki), rec)]
+        for idx, v in enumerate((gr, gi, pr, pi, kr, ki)):
+            back_ref[k, idx] = v
         Gr, Gi = g_ref[k, 4], g_ref[k, 5]
         Pr, Pi = g_ref[k, 6], g_ref[k, 7]
         Qr, Qi = g_ref[k, 8], g_ref[k, 9]
@@ -158,7 +154,8 @@
         nr, ni = cmul(Gr, Gi, kr, ki)
         kr, ki = nr + yr, ni + yi
     bwd_tot = (gr, gi, pr, pi, kr, ki)
-    bwd_me = rec
+    mine_back = back_ref[me]
+    bwd_me = [mine_back[idx] for idx in range(6)]
     for idx, v in enumerate(fwd_tot + bwd_tot):
         for s in range(tot_ref.shape[0]):
             tot_ref[s, idx] = v
@@ -303,7 +300,8 @@
         ),
         in_specs=[pl.BlockSpec(memory_space=SMEM), pl.BlockSpec(memory_space=VMEM)],
         out_specs=(pl.BlockSpec(memory_space=VMEM), pl.BlockSpec(memory_space=VMEM)),
-        scratch_shapes=[pltpu.VMEM((count,) + mode_shape, jnp.float32) for _ in range(4)],
+        scratch_shapes=[pltpu.VMEM((count,) + mode_shape, jnp.float32) for _ in range(4)]
+        + [pltpu.VMEM((count, 6) + mode_shape, jnp.float32)],
     )(blk_index.astype(jnp.int32).reshape(1), gathered)
 
     seg_tot = gathered_over(tot, "seg")

time: 58.6 us -> 58.6 us (level)
  no operation moved by 1% of the time
where the time goes in v11:
time: 58.6 us; the launch traced here: 58.1 us
  blocking collectives  40.1 us (68%)
  Pallas kernels  17.4 us (30%)
  between operations  0.65 us (1%)
    all_to_all x2, blocking collectives, gathered_over(): return lax.all_to_all(spread, axis, 0, 0, tiled=False)  40.1 us
    pallas_call x1, Pallas kernels, on_device(): pl.pallas_call(final_kernel, out_shape=(out_block, out_block), in_specs=[...  10.1 us
    pallas_call x1, Pallas kernels, on_device(): pl.pallas_call(summary_kernel, out_shape=jax.ShapeDtypeStruct((lax.axis_s...  5.28 us
    pallas_call x1, Pallas kernels, on_device(): pl.pallas_call(segment_kernel, out_shape=(jax.ShapeDtypeStruct((lax.axis_...  2.04 us

profile of v11, /device:TPU:1, one launch (start us, length us, event | category | flops | bytes accessed | tf_op | source)
XLA Modules:
  0.0 58.1 jit_solution(15643980406743191926)
XLA Ops:
  0.6 5.3 %shard_map.104 = f32[32,10,4,128]{3,2,1,0:T(4,128)} custom-call(s32[256]{0:T(256)} %flags_ref.3, s32[1]{0:T(128)} %bitcast.last_ref, f32[4,256,256]{2,1,0:T(8,128)} %w_ref.3, f32[4,256,256]{2,1,0:T(8,128)} %d_ref.3, f32[1,4,128]{2,1,0:T(4,128)} %fd_hbm.3, f32[1,4,128]{2,1,0:T(4,128)} %bd_hbm.3, f32[1,4,128]{2,1,0:T(4,128)} %th_hbm.3), custom_call_target="tpu_custom_call" | custom-call | tf_op jit(solution)/shard_map/pallas_call | solution.py:284
  5.9 21.6 %all_to_all.10.g_ref = f32[32,10,4,128]{3,2,1,0:T(4,128)} all-to-all(f32[32,10,4,128]{3,2,1,0:T(4,128)} %shard_map.104), channel_id=1, replica_groups=mesh['seg'=8,'blk'=32] {'blk'}, dimensions={0} | all-to-all | bytes 1310720 | tf_op jit(solution)/shard_map/all_to_all | solution.py:258
  27.5 2.0 %shard_map.105 = (f32[8,10,4,128]{3,2,1,0:T(4,128)}, f32[10,4,128]{2,1,0:T(4,128)}) custom-call(s32[1]{0:T(128)} %bitcast.2.me_ref, f32[32,10,4,128]{3,2,1,0:T(4,128)} %all_to_all.10.g_ref), custom_call_target="tpu_custom_call" | custom-call | tf_op jit(solution)/shard_map/pallas_call | solution.py:295
  29.6 18.5 %all_to_all.11.tot_ref = f32[8,10,4,128]{3,2,1,0:T(4,128)} all-to-all(f32[8,10,4,128]{3,2,1,0:T(4,128)} %get-tuple-element.4), channel_id=1, replica_groups=mesh['seg'=8,'blk'=32] {'seg'}, dimensions={0} | all-to-all | bytes 327680 | tf_op jit(solution)/shard_map/all_to_all | solution.py:258
  48.0 10.1 %shard_map.106 = (bf16[4,256,256]{2,1,0:T(8,128)(2,1)}, bf16[4,256,256]{2,1,0:T(8,128)(2,1)}) custom-call(s32[256]{0:T(256)} %flags_ref.3, s32[1]{0:T(128)} %bitcast.last_ref, s32[1]{0:T(128)} %bitcast.1.myseg_ref, f32[8,10,4,128]{3,2,1,0:T(4,128)} %all_to_all.11.tot_ref, f32[10,4,128]{2,1,0:T(4,128)} %get-tuple-element.5.mine_ref, f32[2,4,128]{2,1,0:T(4,128)} %prior_ref.1, ...), custom_call_target="tpu_custom_call" | custom-call | tf_op jit(solution)/shard_map/pallas_call | solution.py:309

commit v12 on v6

--- a/solution.py
+++ b/solution.py
@@ -167,8 +167,8 @@
 
 
 def final_kernel(flags_ref, last_ref, myseg_ref, tot_ref, mine_ref, prior_ref, w_ref, d_ref, e_hbm,
-                 o_hbm, fd_hbm, bd_hbm, th_hbm, states_ref, fitted_ref, u_ref, m_r, m_i, out_ref, e_ref,
-                 o_ref, rate_ref, sems):
+                 o_hbm, fd_hbm, bd_hbm, th_hbm, states_hbm, fitted_hbm, u_ref, m_r, m_i, out_ref, e_ref,
+                 o_ref, rate_ref, states_ref, fitted_ref, sems):
     e_copy = pltpu.make_async_copy(e_hbm, e_ref, sems.at[0])
     o_copy = pltpu.make_async_copy(o_hbm, o_ref, sems.at[1])
     e_copy.start()
@@ -249,12 +249,19 @@
     e_copy.wait()
     o_copy.wait()
     contract = (((1,), (1,)), ((), ()))
+    written = []
     for a in range(e_ref.shape[0]):
         stacked = out_ref[:, a, :]
         states = dot3(e_ref[a], stacked, contract)
         states_ref[a] = states.astype(states_ref.dtype)
         seen = dot3(o_ref[a], stacked, contract)
         fitted_ref[a] = (d_ref[a] - seen).astype(fitted_ref.dtype)
+        for c in (pltpu.make_async_copy(states_ref.at[a], states_hbm.at[a], sems.at[5 + 2 * a]),
+                  pltpu.make_async_copy(fitted_ref.at[a], fitted_hbm.at[a], sems.at[6 + 2 * a])):
+            c.start()
+            written.append(c)
+    for c in written:
+        c.wait()
 
 
 def gathered_over(spread, axis):
@@ -313,12 +320,14 @@
         out_shape=(out_block, out_block),
         in_specs=[pl.BlockSpec(memory_space=SMEM)] * 3 + [pl.BlockSpec(memory_space=VMEM)] * 5
         + [pl.BlockSpec(memory_space=pl.ANY)] * 5,
-        out_specs=(pl.BlockSpec(memory_space=VMEM), pl.BlockSpec(memory_space=VMEM)),
+        out_specs=(pl.BlockSpec(memory_space=pl.ANY), pl.BlockSpec(memory_space=pl.ANY)),
         scratch_shapes=[pltpu.VMEM(u_shape, jnp.float32)]
         + [pltpu.VMEM((steps,) + mode_shape, jnp.float32) for _ in range(2)]
         + [pltpu.VMEM(u_shape, jnp.float32)]
         + [pltpu.VMEM(eigenbasis_columns.shape, jnp.float32) for _ in range(2)]
-        + [rate_scratch, pltpu.SemaphoreType.DMA((5,))],
+        + [rate_scratch]
+        + [pltpu.VMEM(sampled_data.shape, jnp.bfloat16) for _ in range(2)]
+        + [pltpu.SemaphoreType.DMA((13,))],
     )(flags, last, seg_index.astype(jnp.int32).reshape(1), seg_tot, mine, prior_expectation,
       update_weights, sampled_data, eigenbasis_columns, measuring_operator, *rates)
     return (states, fitted)

time: 58.6 us -> 58.4 us (level)
  no operation moved by 1% of the time
where the time goes in v12:
time: 58.4 us; the launch traced here: 58 us
  blocking collectives  40.1 us (69%)
  Pallas kernels  17.3 us (30%)
  between operations  0.65 us (1%)
    all_to_all x2, blocking collectives, gathered_over(): return lax.all_to_all(spread, axis, 0, 0, tiled=False)  40.1 us
    pallas_call x1, Pallas kernels, on_device(): pl.pallas_call(final_kernel, out_shape=(out_block, out_block), in_specs=[...  9.93 us
    pallas_call x1, Pallas kernels, on_device(): pl.pallas_call(summary_kernel, out_shape=jax.ShapeDtypeStruct((lax.axis_s...  5.28 us
    pallas_call x1, Pallas kernels, on_device(): pl.pallas_call(segment_kernel, out_shape=(jax.ShapeDtypeStruct((lax.axis_...  2.06 us

profile of v12, /device:TPU:1, one launch (start us, length us, event | category | flops | bytes accessed | tf_op | source)
XLA Modules:
  0.0 58.0 jit_solution(16681820650047009494)
XLA Ops:
  0.6 5.3 %shard_map.104 = f32[32,10,4,128]{3,2,1,0:T(4,128)} custom-call(s32[256]{0:T(256)} %flags_ref.3, s32[1]{0:T(128)} %bitcast.last_ref, f32[4,256,256]{2,1,0:T(8,128)} %w_ref.3, f32[4,256,256]{2,1,0:T(8,128)} %d_ref.3, f32[1,4,128]{2,1,0:T(4,128)} %fd_hbm.3, f32[1,4,128]{2,1,0:T(4,128)} %bd_hbm.3, f32[1,4,128]{2,1,0:T(4,128)} %th_hbm.3), custom_call_target="tpu_custom_call" | custom-call | tf_op jit(solution)/shard_map/pallas_call | solution.py:294
  5.9 21.6 %all_to_all.10.g_ref = f32[32,10,4,128]{3,2,1,0:T(4,128)} all-to-all(f32[32,10,4,128]{3,2,1,0:T(4,128)} %shard_map.104), channel_id=1, replica_groups=mesh['seg'=8,'blk'=32] {'blk'}, dimensions={0} | all-to-all | bytes 1310720 | tf_op jit(solution)/shard_map/all_to_all | solution.py:268
  27.5 2.1 %shard_map.105 = (f32[8,10,4,128]{3,2,1,0:T(4,128)}, f32[10,4,128]{2,1,0:T(4,128)}) custom-call(s32[1]{0:T(128)} %bitcast.2.me_ref, f32[32,10,4,128]{3,2,1,0:T(4,128)} %all_to_all.10.g_ref), custom_call_target="tpu_custom_call" | custom-call | tf_op jit(solution)/shard_map/pallas_call | solution.py:305
  29.6 18.5 %all_to_all.11.tot_ref = f32[8,10,4,128]{3,2,1,0:T(4,128)} all-to-all(f32[8,10,4,128]{3,2,1,0:T(4,128)} %get-tuple-element.4), channel_id=1, replica_groups=mesh['seg'=8,'blk'=32] {'seg'}, dimensions={0} | all-to-all | bytes 327680 | tf_op jit(solution)/shard_map/all_to_all | solution.py:268
  48.0 9.9 %shard_map.106 = (bf16[4,256,256]{2,1,0:T(8,128)(2,1)}, bf16[4,256,256]{2,1,0:T(8,128)(2,1)}) custom-call(s32[256]{0:T(256)} %flags_ref.3, s32[1]{0:T(128)} %bitcast.last_ref, s32[1]{0:T(128)} %bitcast.1.myseg_ref, f32[8,10,4,128]{3,2,1,0:T(4,128)} %all_to_all.11.tot_ref, f32[10,4,128]{2,1,0:T(4,128)} %get-tuple-element.5.mine_ref, f32[2,4,128]{2,1,0:T(4,128)} %prior_ref.1, ...), custom_call_target="tpu_custom_call" | custom-call | tf_op jit(solution)/shard_map/pallas_call | solution.py:318

commit v13 on v11

--- a/solution.py
+++ b/solution.py
@@ -164,8 +164,8 @@
 
 
 def final_kernel(flags_ref, last_ref, myseg_ref, tot_ref, mine_ref, prior_ref, w_ref, d_ref, e_hbm,
-                 o_hbm, fd_hbm, bd_hbm, th_hbm, states_ref, fitted_ref, u_ref, m_r, m_i, out_ref, e_ref,
-                 o_ref, rate_ref, sems):
+                 o_hbm, fd_hbm, bd_hbm, th_hbm, states_hbm, fitted_hbm, u_ref, m_r, m_i, out_ref, e_ref,
+                 o_ref, rate_ref, states_ref, fitted_ref, sems):
     e_copy = pltpu.make_async_copy(e_hbm, e_ref, sems.at[0])
     o_copy = pltpu.make_async_copy(o_hbm, o_ref, sems.at[1])
     e_copy.start()
@@ -246,12 +246,19 @@
     e_copy.wait()
     o_copy.wait()
     contract = (((1,), (1,)), ((), ()))
+    written = []
     for a in range(e_ref.shape[0]):
         stacked = out_ref[:, a, :]
         states = dot3(e_ref[a], stacked, contract)
         states_ref[a] = states.astype(states_ref.dtype)
         seen = dot3(o_ref[a], stacked, contract)
         fitted_ref[a] = (d_ref[a] - seen).astype(fitted_ref.dtype)
+        for c in (pltpu.make_async_copy(states_ref.at[a], states_hbm.at[a], sems.at[5 + 2 * a]),
+                  pltpu.make_async_copy(fitted_ref.at[a], fitted_hbm.at[a], sems.at[6 + 2 * a])):
+            c.start()
+            written.append(c)
+    for c in written:
+        c.wait()
 
 
 def gathered_over(spread, axis):
@@ -311,12 +318,14 @@
         out_shape=(out_block, out_block),
         in_specs=[pl.BlockSpec(memory_space=SMEM)] * 3 + [pl.BlockSpec(memory_space=VMEM)] * 5
         + [pl.BlockSpec(memory_space=pl.ANY)] * 5,
-        out_specs=(pl.BlockSpec(memory_space=VMEM), pl.BlockSpec(memory_space=VMEM)),
+        out_specs=(pl.BlockSpec(memory_space=pl.ANY), pl.BlockSpec(memory_space=pl.ANY)),
         scratch_shapes=[pltpu.VMEM(u_shape, jnp.float32)]
         + [pltpu.VMEM((steps,) + mode_shape, jnp.float32) for _ in range(2)]
         + [pltpu.VMEM(u_shape, jnp.float32)]
         + [pltpu.VMEM(eigenbasis_columns.shape, jnp.float32) for _ in range(2)]
-        + [rate_scratch, pltpu.SemaphoreType.DMA((5,))],
+        + [rate_scratch]
+        + [pltpu.VMEM(sampled_data.shape, jnp.bfloat16) for _ in range(2)]
+        + [pltpu.SemaphoreType.DMA((13,))],
     )(flags, last, seg_index.astype(jnp.int32).reshape(1), seg_tot, mine, prior_expectation,
       update_weights, sampled_data, eigenbasis_columns, measuring_operator, *rates)
     return (states, fitted)

time: 58.6 us -> 58.4 us (level)
  no operation moved by 1% of the time
where the time goes in v13:
time: 58.4 us; the launch traced here: 58 us
  blocking collectives  40.1 us (69%)
  Pallas kernels  17.2 us (29%)
  between operations  0.65 us (1%)
    all_to_all x2, blocking collectives, gathered_over(): return lax.all_to_all(spread, axis, 0, 0, tiled=False)  40.1 us
    pallas_call x1, Pallas kernels, on_device(): pl.pallas_call(final_kernel, out_shape=(out_block, out_block), in_specs=[...  9.93 us
    pallas_call x1, Pallas kernels, on_device(): pl.pallas_call(summary_kernel, out_shape=jax.ShapeDtypeStruct((lax.axis_s...  5.28 us
    pallas_call x1, Pallas kernels, on_device(): pl.pallas_call(segment_kernel, out_shape=(jax.ShapeDtypeStruct((lax.axis_...  2.04 us

profile of v13, /device:TPU:1, one launch (start us, length us, event | category | flops | bytes accessed | tf_op | source)
XLA Modules:
  0.0 58.0 jit_solution(15784303504873645804)
XLA Ops:
  0.6 5.3 %shard_map.104 = f32[32,10,4,128]{3,2,1,0:T(4,128)} custom-call(s32[256]{0:T(256)} %flags_ref.3, s32[1]{0:T(128)} %bitcast.last_ref, f32[4,256,256]{2,1,0:T(8,128)} %w_ref.3, f32[4,256,256]{2,1,0:T(8,128)} %d_ref.3, f32[1,4,128]{2,1,0:T(4,128)} %fd_hbm.3, f32[1,4,128]{2,1,0:T(4,128)} %bd_hbm.3, f32[1,4,128]{2,1,0:T(4,128)} %th_hbm.3), custom_call_target="tpu_custom_call" | custom-call | tf_op jit(solution)/shard_map/pallas_call | solution.py:291
  5.9 21.6 %all_to_all.10.g_ref = f32[32,10,4,128]{3,2,1,0:T(4,128)} all-to-all(f32[32,10,4,128]{3,2,1,0:T(4,128)} %shard_map.104), channel_id=1, replica_groups=mesh['seg'=8,'blk'=32] {'blk'}, dimensions={0} | all-to-all | bytes 1310720 | tf_op jit(solution)/shard_map/all_to_all | solution.py:265
  27.5 2.0 %shard_map.105 = (f32[8,10,4,128]{3,2,1,0:T(4,128)}, f32[10,4,128]{2,1,0:T(4,128)}) custom-call(s32[1]{0:T(128)} %bitcast.2.me_ref, f32[32,10,4,128]{3,2,1,0:T(4,128)} %all_to_all.10.g_ref), custom_call_target="tpu_custom_call" | custom-call | tf_op jit(solution)/shard_map/pallas_call | solution.py:302
  29.6 18.5 %all_to_all.11.tot_ref = f32[8,10,4,128]{3,2,1,0:T(4,128)} all-to-all(f32[8,10,4,128]{3,2,1,0:T(4,128)} %get-tuple-element.4), channel_id=1, replica_groups=mesh['seg'=8,'blk'=32] {'seg'}, dimensions={0} | all-to-all | bytes 327680 | tf_op jit(solution)/shard_map/all_to_all | solution.py:265
  48.0 9.9 %shard_map.106 = (bf16[4,256,256]{2,1,0:T(8,128)(2,1)}, bf16[4,256,256]{2,1,0:T(8,128)(2,1)}) custom-call(s32[256]{0:T(256)} %flags_ref.3, s32[1]{0:T(128)} %bitcast.last_ref, s32[1]{0:T(128)} %bitcast.1.myseg_ref, f32[8,10,4,128]{3,2,1,0:T(4,128)} %all_to_all.11.tot_ref, f32[10,4,128]{2,1,0:T(4,128)} %get-tuple-element.5.mine_ref, f32[2,4,128]{2,1,0:T(4,128)} %prior_ref.1, ...), custom_call_target="tpu_custom_call" | custom-call | tf_op jit(solution)/shard_map/pallas_call | solution.py:316
